TPU v7x, 512 devices: a whole 4x4x16 slice. The times are simulated.
512 devices in a mesh: seg: 32 (over z, core), row: 16 (over x, y).
Axes of the slice: x: 4, y: 4, z: 16, core: 2. Of those that a mesh axis runs over, the one named last changes fastest.
Arguments:
- basis: bfloat16 [32, 8192, 1024], P('seg', 'row'), may hold values from -6 to 6
- arriving: bfloat16 [8192, 1024], P('row'), may hold values from -6 to 6
- blocks: bfloat16 [32, 8192, 256], P('seg', 'row'), may hold values from -8 to 8
- pattern: int32 [32, 128, 4], P('seg', 'row'), may hold values from 0 to 127, as said below
- growth: float32 [32, 1024], P('seg'), may hold values from -6 to 6
Outputs:
- next_basis: bfloat16 [32, 8192, 1024], P('seg', 'row')
- next_growth: float32 [32, 1024], P('seg')
Inputs may be any that keep to these rules, and one draw needn't show every extreme that they name: `pattern`: entry 0 of block row r is r itself; entry 1 is the block 4 positions before or after r on the cycle of 128 blocks; the other entries are distinct blocks fewer than 4 positions from r and not r.
All inputs are finite; a program needn't handle non-finite values.
Results may differ from a plain program's by a relative error of at most 0.0053.
Values may be sent and summed in bfloat16 or wider, within the bound.
No kernel may reach another device: no remote copies, remote signals or barrier semaphores. Data moves between devices by JAX's collectives and lax.ppermute only.
A program may use at most 128 MiB of HBM per device.

v0:
```python
import jax
import jax.numpy as jnp
from jax import lax
from jax.sharding import PartitionSpec as P

BS = 64
NB = 4
REACH = 4
PANEL = 128
HIGHEST = lax.Precision.HIGHEST


def padded_2(block, sides, width):
    for axis, dim in sides:
        count = lax.axis_size(axis)
        forward = [(i, i + 1) for i in range(count - 1)]
        forward.append((count - 1, 0))
        backward = [(target, source) for source, target in forward]
        low = lax.ppermute(
            lax.slice_in_dim(block, block.shape[dim] - width, None, axis=dim), axis, forward
        )
        high = lax.ppermute(lax.slice_in_dim(block, 0, width, axis=dim), axis, backward)
        block = jnp.concatenate([low, block, high], axis=dim)
    return block


def shifted(array, axis, by):
    length = lax.axis_size(axis)
    pairs = [(i, i + by) for i in range(length) if 0 <= i + by < length]
    return lax.ppermute(array, axis, pairs)


def times_t(a, b):
    return lax.dot_general(
        a, b, (((1,), (1,)), ((), ())), precision=HIGHEST, preferred_element_type=jnp.float32
    )


def body(basis, arriving, blocks, pattern, growth):
    row_count = basis.shape[1]
    col_count = basis.shape[2]
    row_blocks = row_count // BS
    total_blocks = row_blocks * lax.axis_size("row")
    padded = padded_2(basis[0], (("row", 0),), REACH * BS)
    tile_stack = padded.reshape(row_blocks + 2 * REACH, BS, col_count)
    local_ids = jnp.arange(row_blocks, dtype=jnp.int32)
    own_blocks = lax.axis_index("row") * row_blocks + local_ids
    offsets = (pattern[0] - own_blocks[:, None] + REACH) % total_blocks
    picked = jnp.take(tile_stack, local_ids[:, None] + offsets, axis=0)
    values = blocks[0].reshape(row_blocks, BS, NB, BS)
    propagated = jnp.einsum("rinj,rnjk->rik", values, picked, preferred_element_type=jnp.float32)
    propagated = propagated.reshape(row_count, col_count).astype(jnp.bfloat16)
    wide_rows = propagated.astype(jnp.float32)
    scale = 1.0 / (row_count * lax.axis_size("row"))

    partial_value = lax.dot_general(
        propagated, propagated, (((0,), (0,)), ((), ())), preferred_element_type=jnp.float32
    )
    gram_matrix = lax.psum(partial_value, "row") * scale

    width = PANEL
    panels = col_count // width
    eye = jnp.eye(width, dtype=jnp.float32)
    columns = []
    solved = []
    logs = []
    for k in range(panels):
        low = k * width
        panel = gram_matrix[low:, low:low + width]
        if k:
            left = jnp.concatenate(
                [column[low - j * width:] for j, column in enumerate(columns)], axis=1
            )
            panel = panel - times_t(left, left[:width])
        diag = jnp.linalg.cholesky(panel[:width])
        inverse = lax.linalg.triangular_solve(diag, eye, left_side=True, lower=True)
        logs.append(jnp.log(jnp.sum(diag * eye, axis=0)))
        if low + width < col_count:
            below = times_t(panel[width:], inverse)
            columns.append(jnp.concatenate([diag, below], axis=0))
        else:
            columns.append(diag)
        rhs = wide_rows[:, low:low + width]
        if k:
            rhs = rhs - times_t(jnp.concatenate(solved, axis=1), left[:width])
        solved.append(times_t(rhs, inverse))

    next_growth = growth + jnp.concatenate(logs)[None, :]
    renewed = jnp.concatenate(solved, axis=1)
    first_section = lax.axis_index("seg") == 0
    received = shifted(renewed.astype(jnp.bfloat16)[None], "seg", 1)
    next_basis = jnp.where(first_section, arriving[None], received)
    return (next_basis, next_growth)


def solution(mesh):
    return jax.shard_map(
        body,
        mesh=mesh,
        in_specs=(
            P("seg", "row", None),
            P("row", None),
            P("seg", "row", None),
            P("seg", "row", None),
            P("seg", None),
        ),
        out_specs=(P("seg", "row", None), P("seg", None)),
        check_vma=False,
    )
```

profile of v0, /device:TPU:1, one launch (start us, length us, event | category | flops | bytes accessed | tf_op | source)
XLA Modules:
  0.0 474.2 jit_solution(18274408927882765046)
XLA Ops:
  8.6 4.0 collective-permute-start
  12.6 5.6 %collective-permute-start.1 = (bf16[256,1024]{1,0:T(8,128)(2,1)S(1)}, bf16[256,1024]{1,0:T(8,128)(2,1)S(1)}, u32[]{:S(2)}, u32[]{:S(2)}) collective-permute-start(bf16[256,1024]{1,0:T(8,128)(2,1)S(1)} %get-tuple-element.9), channel_id=1, source_target_pairs={{1,0},{2,1},{3,2},{4,3},{5,4},{6,5},{7,6},{8,7},{9,8},{10,9},{11,1... | collective-permute-start | bytes 1572872 | tf_op jit(solution)/shard_map/ppermute | solution.py:22
  39.4 140.7 %all-reduce.2.cloned.1.call-done = f32[1024,1024]{0,1:T(8,128)} async-done(((f32[1024,1024]{0,1:T(8,128)}), f32[1024,1024]{0,1:T(8,128)}) %all-reduce.2.cloned.1.call-update) | async-done | bytes 4194320 | tf_op jit(solution)/shard_map/psum | solution.py:59
  185.6 11.7 %cholesky.134 = f32[128,128]{1,0:T(8,128)S(1)} custom-call(f32[128,128]{1,0:T(8,128)S(1)} %fusion.90), custom_call_target="Cholesky" | custom-call | tf_op jit(solution)/shard_map/jit(cholesky)/cholesky | solution.py:75
  198.7 9.8 %custom-call.12 = f32[1,128,128]{1,2,0:T(8,128)S(1)} custom-call(f32[1,128,128]{2,1,0:T(8,128)S(1)} %get-tuple-element.42), custom_call_target="InvertDiagBlocksLowerTriangular" | custom-call | tf_op jit(solution)/shard_map/triangular_solve/custom-call.0 | solution.py:76
  214.3 11.7 %cholesky.145 = f32[128,128]{1,0:T(8,128)S(1)} custom-call(f32[128,128]{1,0:T(8,128)S(1)} %fusion.88), custom_call_target="Cholesky" | custom-call | tf_op jit(solution)/shard_map/jit(cholesky)/cholesky | solution.py:75
  227.5 9.8 %custom-call.13 = f32[1,128,128]{1,2,0:T(8,128)S(1)} custom-call(f32[1,128,128]{2,1,0:T(8,128)S(1)} %get-tuple-element.40), custom_call_target="InvertDiagBlocksLowerTriangular" | custom-call | tf_op jit(solution)/shard_map/triangular_solve/custom-call.0 | solution.py:76
  251.4 11.7 %cholesky.156 = f32[128,128]{1,0:T(8,128)S(1)} custom-call(f32[128,128]{1,0:T(8,128)S(1)} %fusion.86), custom_call_target="Cholesky" | custom-call | tf_op jit(solution)/shard_map/jit(cholesky)/cholesky | solution.py:75
  264.5 9.8 %custom-call.14 = f32[1,128,128]{1,2,0:T(8,128)S(1)} custom-call(f32[1,128,128]{2,1,0:T(8,128)S(1)} %get-tuple-element.38), custom_call_target="InvertDiagBlocksLowerTriangular" | custom-call | tf_op jit(solution)/shard_map/triangular_solve/custom-call.0 | solution.py:76
  284.4 11.7 %cholesky.167 = f32[128,128]{1,0:T(8,128)S(1)} custom-call(f32[128,128]{1,0:T(8,128)S(1)} %fusion.84), custom_call_target="Cholesky" | custom-call | tf_op jit(solution)/shard_map/jit(cholesky)/cholesky | solution.py:75
  298.0 9.8 %custom-call.15 = f32[1,128,128]{1,2,0:T(8,128)S(1)} custom-call(f32[1,128,128]{2,1,0:T(8,128)S(1)} %get-tuple-element.36), custom_call_target="InvertDiagBlocksLowerTriangular" | custom-call | tf_op jit(solution)/shard_map/triangular_solve/custom-call.0 | solution.py:76
  317.7 11.7 %cholesky.178 = f32[128,128]{1,0:T(8,128)S(1)} custom-call(f32[128,128]{1,0:T(8,128)S(1)} %fusion.82), custom_call_target="Cholesky" | custom-call | tf_op jit(solution)/shard_map/jit(cholesky)/cholesky | solution.py:75
  331.4 9.8 %custom-call.16 = f32[1,128,128]{1,2,0:T(8,128)S(1)} custom-call(f32[1,128,128]{2,1,0:T(8,128)S(1)} %get-tuple-element.34), custom_call_target="InvertDiagBlocksLowerTriangular" | custom-call | tf_op jit(solution)/shard_map/triangular_solve/custom-call.0 | solution.py:76
  352.0 11.7 %cholesky.189 = f32[128,128]{1,0:T(8,128)S(1)} custom-call(f32[128,128]{1,0:T(8,128)S(1)} %fusion.80), custom_call_target="Cholesky" | custom-call | tf_op jit(solution)/shard_map/jit(cholesky)/cholesky | solution.py:75
  365.7 9.8 %custom-call.17 = f32[1,128,128]{1,2,0:T(8,128)S(1)} custom-call(f32[1,128,128]{2,1,0:T(8,128)S(1)} %get-tuple-element.32), custom_call_target="InvertDiagBlocksLowerTriangular" | custom-call | tf_op jit(solution)/shard_map/triangular_solve/custom-call.0 | solution.py:76
  379.0 11.7 %cholesky.200 = f32[128,128]{1,0:T(8,128)S(1)} custom-call(f32[128,128]{1,0:T(8,128)S(1)} %fusion.78), custom_call_target="Cholesky" | custom-call | tf_op jit(solution)/shard_map/jit(cholesky)/cholesky | solution.py:75
  392.6 9.8 %custom-call.18 = f32[1,128,128]{1,2,0:T(8,128)S(1)} custom-call(f32[1,128,128]{2,1,0:T(8,128)S(1)} %get-tuple-element.30), custom_call_target="InvertDiagBlocksLowerTriangular" | custom-call | tf_op jit(solution)/shard_map/triangular_solve/custom-call.0 | solution.py:76
  406.4 11.9 %cholesky.211 = f32[128,128]{1,0:T(8,128)S(1)} custom-call(f32[128,128]{1,0:T(8,128)S(1)} %fusion.76), custom_call_target="Cholesky" | custom-call | tf_op jit(solution)/shard_map/jit(cholesky)/cholesky | solution.py:75
  420.2 9.8 %custom-call.19 = f32[1,128,128]{1,2,0:T(8,128)S(1)} custom-call(f32[1,128,128]{2,1,0:T(8,128)S(1)} %get-tuple-element.28), custom_call_target="InvertDiagBlocksLowerTriangular" | custom-call | tf_op jit(solution)/shard_map/triangular_solve/custom-call.0 | solution.py:76
  435.5 3.8 convolution_subtract_fusion.4
  440.4 4.1 convolution_subtract_fusion.7
  445.0 4.4 convolution_subtract_fusion.3
  449.8 4.1 collective-permute-start.2
  454.7 10.9 %collective-permute-done.2 = bf16[1,512,1024]{1,2,0:T(8,128)(2,1)S(1)} collective-permute-done((bf16[1,512,1024]{1,2,0:T(8,128)(2,1)S(1)}, bf16[1,512,1024]{1,2,0:T(8,128)(2,1)S(1)}, u32[]{:S(2)}, u32[]{:S(2)}) %collective-permute-start.2) | collective-permute-done | bytes 1048608 | tf_op jit(solution)/shard_map/ppermute | solution.py:30
  (215 shorter events, 109.1 us)
Async XLA Ops:
  7.2 17.9 %copy-start.14 = (bf16[1,512,1024]{2,1,0:T(8,128)(2,1)S(1)}, bf16[1,512,1024]{2,1,0:T(8,128)(2,1)}, u32[]{:S(2)}) copy-start(bf16[1,512,1024]{2,1,0:T(8,128)(2,1)} %param.8) | copy-start | bytes 3145732
  7.2 11.0 %copy-start.30 = (s32[1,8,4]{1,2,0:T(4,128)S(1)}, s32[1,8,4]{1,2,0:T(4,128)}, u32[]{:S(2)}) copy-start(s32[1,8,4]{1,2,0:T(4,128)} %param.11) | copy-start | bytes 388
  7.2 11.3 %copy-start.28 = (bf16[1,512,256]{2,1,0:T(8,128)(2,1)S(1)}, bf16[1,512,256]{2,1,0:T(8,128)(2,1)}, u32[]{:S(2)}) copy-start(bf16[1,512,256]{2,1,0:T(8,128)(2,1)} %param.10) | copy-start | bytes 786436
  7.2 172.9 %all-reduce.2.cloned.1.call-start = ((), (), s32[]{:S(2)}) async-start(), calls=%async_computation | async-start | bytes 8388608 | tf_op jit(solution)/shard_map/psum | solution.py:59
  8.6 14.2 %collective-permute-start = (bf16[256,1024]{1,0:T(8,128)(2,1)S(1)}, bf16[256,1024]{1,0:T(8,128)(2,1)S(1)}, u32[]{:S(2)}, u32[]{:S(2)}) collective-permute-start(bf16[256,1024]{1,0:T(8,128)(2,1)S(1)} %get-tuple-element.8), channel_id=1, source_target_pairs={{0,1},{1,2},{2,3},{3,4},{4,5},{5,6},{6,7},{7,8},{8,9},{9,10},{10,1... | collective-permute-start | bytes 1572872 | tf_op jit(solution)/shard_map/ppermute | solution.py:19
  12.6 11.7 %collective-permute-start.1 = (bf16[256,1024]{1,0:T(8,128)(2,1)S(1)}, bf16[256,1024]{1,0:T(8,128)(2,1)S(1)}, u32[]{:S(2)}, u32[]{:S(2)}) collective-permute-start(bf16[256,1024]{1,0:T(8,128)(2,1)S(1)} %get-tuple-element.9), channel_id=1, source_target_pairs={{1,0},{2,1},{3,2},{4,3},{5,4},{6,5},{7,6},{8,7},{9,8},{10,9},{11,1... | collective-permute-start | bytes 1572872 | tf_op jit(solution)/shard_map/ppermute | solution.py:22
  32.7 6.4 %copy-start.21 = (bf16[8,1024,64]{1,2,0:T(8,128)(2,1)}, bf16[8,1024,64]{1,2,0:T(8,128)(2,1)S(1)}, u32[]{:S(2)}) copy-start(bf16[8,1024,64]{1,2,0:T(8,128)(2,1)S(1)} %bitcast_convert_fusion) | copy-start | bytes 3145732
  214.2 23.2 %copy-start.18 = (f32[896,128]{0,1:T(8,128)}, f32[896,128]{0,1:T(8,128)S(1)}, u32[]{:S(2)}) copy-start(f32[896,128]{0,1:T(8,128)S(1)} %convolution_subtract_fusion) | copy-start | bytes 1376260
  239.9 6.1 %copy-start.4 = (f32[768,128]{0,1:T(8,128)S(1)}, f32[768,128]{0,1:T(8,128)}, u32[]{:S(2)}) copy-start(f32[768,128]{0,1:T(8,128)} %slice.265) | copy-start | bytes 1179652
  248.7 32.5 %copy-start.1 = (f32[512,128]{0,1:T(8,128)}, f32[512,128]{0,1:T(8,128)S(1)}, u32[]{:S(2)}) copy-start(f32[512,128]{0,1:T(8,128)S(1)} %get-tuple-element.46) | copy-start | bytes 786436
  308.1 5.6 %copy-start.2 = (f32[512,128]{0,1:T(8,128)S(1)}, f32[512,128]{0,1:T(8,128)}, u32[]{:S(2)}) copy-start(f32[512,128]{0,1:T(8,128)} %copy-done.1) | copy-start | bytes 786436
  316.7 30.6 %copy-start.23 = (f32[512,128]{0,1:T(8,128)S(1)}, f32[512,128]{0,1:T(8,128)}, u32[]{:S(2)}) copy-start(f32[512,128]{0,1:T(8,128)} %copy-done.22) | copy-start | bytes 786436
  376.8 53.5 %copy-start.25 = (f32[512,128]{1,0:T(8,128)S(1)}, f32[512,128]{1,0:T(8,128)}, u32[]{:S(2)}) copy-start(f32[512,128]{1,0:T(8,128)} %convolution_subtract_fusion.10) | copy-start | bytes 786436
  378.9 52.5 %copy-start.3 = (f32[512,128]{0,1:T(8,128)S(1)}, f32[512,128]{0,1:T(8,128)}, u32[]{:S(2)}) copy-start(f32[512,128]{0,1:T(8,128)} %copy-done.1) | copy-start | bytes 786436
  403.4 29.0 %copy-start.13 = (f32[512,128]{0,1:T(8,128)S(1)}, f32[512,128]{0,1:T(8,128)}, u32[]{:S(2)}) copy-start(f32[512,128]{0,1:T(8,128)} %copy-done.11) | copy-start | bytes 786436
  406.3 27.1 %copy-start.17 = (f32[512,128]{0,1:T(8,128)S(1)}, f32[512,128]{0,1:T(8,128)}, u32[]{:S(2)}) copy-start(f32[512,128]{0,1:T(8,128)} %copy-done.16) | copy-start | bytes 786436
  444.9 9.1 %copy-start.32 = (f32[128]{0:T(128)S(1)}, f32[128]{0:T(128)}, u32[]{:S(2)}) copy-start(f32[128]{0:T(128)} %get-tuple-element.35) | copy-start | bytes 1540
  444.9 9.1 %copy-start.33 = (f32[128]{0:T(128)S(1)}, f32[128]{0:T(128)}, u32[]{:S(2)}) copy-start(f32[128]{0:T(128)} %get-tuple-element.33) | copy-start | bytes 1540
  444.9 9.1 %copy-start.34 = (f32[128]{0:T(128)S(1)}, f32[128]{0:T(128)}, u32[]{:S(2)}) copy-start(f32[128]{0:T(128)} %get-tuple-element.31) | copy-start | bytes 1540
  444.9 9.1 %copy-start.35 = (f32[128]{0:T(128)S(1)}, f32[128]{0:T(128)}, u32[]{:S(2)}) copy-start(f32[128]{0:T(128)} %get-tuple-element.29) | copy-start | bytes 1540
  444.9 9.1 %copy-start.36 = (f32[128]{0:T(128)S(1)}, f32[128]{0:T(128)}, u32[]{:S(2)}) copy-start(f32[128]{0:T(128)} %get-tuple-element.27) | copy-start | bytes 1540
  444.9 9.1 %copy-start.31 = (f32[1,1024]{1,0:T(1,128)S(1)}, f32[1,1024]{1,0:T(1,128)}, u32[]{:S(2)}) copy-start(f32[1,1024]{1,0:T(1,128)} %param.12) | copy-start | bytes 12292
  445.0 20.7 %copy-start.10 = (bf16[512,1024]{0,1:T(8,128)(2,1)S(1)}, bf16[512,1024]{0,1:T(8,128)(2,1)}, u32[]{:S(2)}) copy-start(bf16[512,1024]{0,1:T(8,128)(2,1)} %copy.28) | copy-start | bytes 3145732
  449.8 15.8 %collective-permute-start.2 = (bf16[1,512,1024]{1,2,0:T(8,128)(2,1)S(1)}, bf16[1,512,1024]{1,2,0:T(8,128)(2,1)S(1)}, u32[]{:S(2)}, u32[]{:S(2)}) collective-permute-start(bf16[1,512,1024]{1,2,0:T(8,128)(2,1)S(1)} %fusion.7), channel_id=1, source_target_pairs={{0,16},{16,32},{32,48},{48,64},{64,80},{80,96},{96,112},{112,128},... | collective-permute-start | bytes 3145736 | tf_op jit(solution)/shard_map/ppermute | solution.py:30
  (17 other events, 64.4 us)
Sparse Core Ops, SparseCore 0:
  36.1 143.8 all-reduce.1
where the time goes:
time: 478 us; the launch traced here: 474 us
  other arithmetic  195 us (41%)
  waiting for transfers between devices  156 us (33%)
  matrix products  60.6 us (13%)
  local copies, waits for them, and re-layouts  33.5 us (7%)
  between operations  15.3 us (3%)
  starting transfers between devices  13.7 us (3%)
    psum x1, waiting for transfers between devices, body(): gram_matrix = lax.psum(partial_value, 'row') * scale  141 us
    another operation x24, other arithmetic, body(): diag = jnp.linalg.cholesky(panel[:width])  99.6 us
    another operation x8, other arithmetic, body(): inverse = lax.linalg.triangular_solve(diag, eye, left_side=True, lower=True)  78.4 us
    dot_general x29, matrix products, times_t(): lax.dot_general(a, b, (((1,), (1,)), ((), ())), precision=HIGHEST, prefer...  51.5 us
    unnamed x104, local copies, waits for them, and re-layouts  22.9 us
    ppermute x1, waiting for transfers between devices, shifted(): return lax.ppermute(array, axis, pairs)  10.9 us
  transfers between devices with their start and end apart: 4, of which 4 were waited for; matrix products, arithmetic and copies ran while one was open for 1% of the time, Pallas kernels for 0%

commit v1 on v0

--- a/solution.py
+++ b/solution.py
@@ -2,6 +2,48 @@
 import jax.numpy as jnp
 from jax import lax
 from jax.sharding import PartitionSpec as P
+from jax.experimental import pallas as pl
+from jax.experimental.pallas import tpu as pltpu
+
+
+def _chol_inv_kernel(a_ref, lt_ref, x_ref):
+    n = a_ref.shape[0]
+    rows = 8
+    nblk = n // rows
+    a = [a_ref[b * rows:(b + 1) * rows, :] for b in range(nblk)]
+    sub = lax.broadcasted_iota(jnp.int32, (rows, n), 0)
+    lane1 = lax.broadcasted_iota(jnp.int32, (1, n), 1)
+    x = [jnp.where(sub + b * rows == lax.broadcasted_iota(jnp.int32, (rows, n), 1), 1.0, 0.0).astype(jnp.float32)
+         for b in range(nblk)]
+    for j in range(n):
+        bj, r = divmod(j, rows)
+        row = a[bj][r:r + 1, :]
+        d = row[:, j:j + 1]
+        s = lax.rsqrt(d)
+        lrow = jnp.where(lane1 >= j, row * s, 0.0)
+        lt_ref[j:j + 1, :] = lrow
+        xrow = x[bj][r:r + 1, :] * s
+        for b in range(bj, nblk):
+            col = a[b][:, j:j + 1] * s
+            if b == bj:
+                keep = sub >= r
+                a[b] = jnp.where(keep, a[b] - col * lrow, a[b])
+                x[b] = jnp.where(sub == r, xrow, jnp.where(sub > r, x[b] - col * xrow, x[b]))
+            else:
+                a[b] = a[b] - col * lrow
+                x[b] = x[b] - col * xrow
+    for b in range(nblk):
+        x_ref[b * rows:(b + 1) * rows, :] = x[b]
+
+
+def chol_inv(a):
+    n = a.shape[0]
+    return pl.pallas_call(
+        _chol_inv_kernel,
+        out_shape=(jax.ShapeDtypeStruct((n, n), jnp.float32), jax.ShapeDtypeStruct((n, n), jnp.float32)),
+        in_specs=[pl.BlockSpec(memory_space=pltpu.VMEM)],
+        out_specs=(pl.BlockSpec(memory_space=pltpu.VMEM), pl.BlockSpec(memory_space=pltpu.VMEM)),
+    )(a)
 
 BS = 64
 NB = 4
@@ -72,8 +114,9 @@
                 [column[low - j * width:] for j, column in enumerate(columns)], axis=1
             )
             panel = panel - times_t(left, left[:width])
-        diag = jnp.linalg.cholesky(panel[:width])
-        inverse = lax.linalg.triangular_solve(diag, eye, left_side=True, lower=True)
+        block = panel[:width]
+        upper, inverse = chol_inv((block + block.T) * 0.5)
+        diag = upper.T
         logs.append(jnp.log(jnp.sum(diag * eye, axis=0)))
         if low + width < col_count:
             below = times_t(panel[width:], inverse)

time: 478 us -> 400 us (0.84)
  other arithmetic: 195 us -> 14.3 us
  Pallas kernels: 0 us -> 99 us
    another operation x32 -> x0, other arithmetic: 178 us -> none  [the longest x24 99.6 us: body(): diag = jnp.linalg.cholesky(panel[:width])]
    pallas_call x0 -> x8, Pallas kernels: none -> 99 us  [chol_inv(): pl.pallas_call(_chol_inv_kernel, out_shape=(jax.ShapeDtypeStruct((n, n),...]
    unnamed x104 -> x114, local copies, waits for them, and re-layouts: 22.9 us -> 22.9 us
where the time goes in v1:
time: 400 us; the launch traced here: 395 us
  waiting for transfers between devices  156 us (39%)
  Pallas kernels  99 us (25%)
  matrix products  59.1 us (15%)
  local copies, waits for them, and re-layouts  38.1 us (10%)
  between operations  15.1 us (4%)
  other arithmetic  14.3 us (4%)
  starting transfers between devices  13.7 us (3%)
    psum x1, waiting for transfers between devices, body(): gram_matrix = lax.psum(partial_value, 'row') * scale  141 us
    pallas_call x8, Pallas kernels, chol_inv(): pl.pallas_call(_chol_inv_kernel, out_shape=(jax.ShapeDtypeStruct((n, n),...  99 us
    dot_general x29, matrix products, times_t(): lax.dot_general(a, b, (((1,), (1,)), ((), ())), precision=HIGHEST, prefer...  52.3 us
    unnamed x114, local copies, waits for them, and re-layouts  22.9 us
    ppermute x1, waiting for transfers between devices, shifted(): return lax.ppermute(array, axis, pairs)  10.8 us
  transfers between devices with their start and end apart: 4, of which 4 were waited for; matrix products, arithmetic and copies ran while one was open for 1% of the time, Pallas kernels for 0%

profile of v1, /device:TPU:1, one launch (start us, length us, event | category | flops | bytes accessed | tf_op | source)
XLA Modules:
  0.0 395.5 jit_solution(4167583485383586310)
XLA Ops:
  8.6 4.0 %collective-permute-start = (bf16[256,1024]{1,0:T(8,128)(2,1)S(1)}, bf16[256,1024]{1,0:T(8,128)(2,1)S(1)}, u32[]{:S(2)}, u32[]{:S(2)}) collective-permute-start(bf16[256,1024]{1,0:T(8,128)(2,1)S(1)} %get-tuple-element.38), channel_id=1, source_target_pairs={{0,1},{1,2},{2,3},{3,4},{4,5},{5,6},{6,7},{7,8},{8,9},{9,10},{10,1... | collective-permute-start | bytes 1572872 | tf_op jit(solution)/shard_map/ppermute | solution.py:61
  12.6 5.6 %collective-permute-start.1 = (bf16[256,1024]{1,0:T(8,128)(2,1)S(1)}, bf16[256,1024]{1,0:T(8,128)(2,1)S(1)}, u32[]{:S(2)}, u32[]{:S(2)}) collective-permute-start(bf16[256,1024]{1,0:T(8,128)(2,1)S(1)} %get-tuple-element.39), channel_id=1, source_target_pairs={{1,0},{2,1},{3,2},{4,3},{5,4},{6,5},{7,6},{8,7},{9,8},{10,9},{11,1... | collective-permute-start | bytes 1572872 | tf_op jit(solution)/shard_map/ppermute | solution.py:64
  19.6 3.2 collective-permute-done
  26.5 2.8 gather_fusion
  29.3 3.5 bitcast_convert_fusion
  32.8 3.3 convolution_bitcast_fusion
  39.4 140.8 %all-reduce.2.cloned.1.call-done = f32[1024,1024]{0,1:T(8,128)} async-done(((f32[1024,1024]{0,1:T(8,128)}), f32[1024,1024]{0,1:T(8,128)}) %all-reduce.2.cloned.1.call-update) | async-done | bytes 4194320 | tf_op jit(solution)/shard_map/psum | solution.py:101
  180.2 2.6 broadcast_multiply_fusion
  186.4 12.3 %shard_map.68 = (f32[128,128]{1,0:T(8,128)}, f32[128,128]{1,0:T(8,128)}) custom-call(f32[128,128]{1,0:T(8,128)} %copy.48.a_ref), custom_call_target="tpu_custom_call" | custom-call | tf_op jit(solution)/shard_map/pallas_call | solution.py:41
  205.1 12.3 %shard_map.69 = (f32[128,128]{1,0:T(8,128)}, f32[128,128]{1,0:T(8,128)}) custom-call(f32[128,128]{1,0:T(8,128)} %copy.52.a_ref), custom_call_target="tpu_custom_call" | custom-call | tf_op jit(solution)/shard_map/pallas_call | solution.py:41
  232.3 12.3 %shard_map.70 = (f32[128,128]{1,0:T(8,128)}, f32[128,128]{1,0:T(8,128)}) custom-call(f32[128,128]{1,0:T(8,128)} %copy.56.a_ref), custom_call_target="tpu_custom_call" | custom-call | tf_op jit(solution)/shard_map/pallas_call | solution.py:41
  249.7 2.2 convolution_subtract_fusion.2
  255.8 12.5 %shard_map.71 = (f32[128,128]{1,0:T(8,128)}, f32[128,128]{1,0:T(8,128)}) custom-call(f32[128,128]{1,0:T(8,128)} %copy.60.a_ref), custom_call_target="tpu_custom_call" | custom-call | tf_op jit(solution)/shard_map/pallas_call | solution.py:41
  274.9 2.5 convolution_subtract_fusion.10
  279.1 12.3 %shard_map.72 = (f32[128,128]{1,0:T(8,128)}, f32[128,128]{1,0:T(8,128)}) custom-call(f32[128,128]{1,0:T(8,128)} %copy.64.a_ref), custom_call_target="tpu_custom_call" | custom-call | tf_op jit(solution)/shard_map/pallas_call | solution.py:41
  300.6 2.2 convolution_subtract_fusion.11
  303.7 12.7 %shard_map.73 = (f32[128,128]{1,0:T(8,128)}, f32[128,128]{1,0:T(8,128)}) custom-call(f32[128,128]{1,0:T(8,128)} %copy.68.a_ref), custom_call_target="tpu_custom_call" | custom-call | tf_op jit(solution)/shard_map/pallas_call | solution.py:41
  322.0 12.3 %shard_map.74 = (f32[128,128]{1,0:T(8,128)}, f32[128,128]{1,0:T(8,128)}) custom-call(f32[128,128]{1,0:T(8,128)} %fusion.67.a_ref), custom_call_target="tpu_custom_call" | custom-call | tf_op jit(solution)/shard_map/pallas_call | solution.py:41
  339.5 12.4 %shard_map.75 = (f32[128,128]{1,0:T(8,128)}, f32[128,128]{1,0:T(8,128)}) custom-call(f32[128,128]{1,0:T(8,128)} %broadcast_multiply_fusion.1.a_ref), custom_call_target="tpu_custom_call" | custom-call | tf_op jit(solution)/shard_map/pallas_call | solution.py:41
  357.1 3.8 convolution_subtract_fusion.4
  362.0 4.1 %convolution_subtract_fusion.7 = f32[512,128]{1,0:T(8,128)S(1)} fusion(f32[512,768]{0,1:T(8,128)} %get-tuple-element.41, f32[256,768]{0,1:T(8,128)} %get-tuple-element.71, f32[512,1024]{1,0:T(8,128)S(1)} %bitcast_convert_fusion.1), kind=kOutput, calls=%fused_computation.16 | convolution fusion | flops 604045312 | bytes 2490368 | tf_op jit(solution)/shard_map/dot_general | solution.py:76
  366.6 4.2 %convolution_subtract_fusion.3 = f32[512,128]{1,0:T(8,128)S(1)} fusion(f32[512,896]{0,1:T(8,128)S(1)} %constant_dynamic-update-slice_fusion.13, f32[128,896]{0,1:T(8,128)} %convolution_dynamic-update-slice_fusion, f32[512,1024]{1,0:T(8,128)S(1)} %bitcast_convert_fusion.1), kind=kOutput, calls=%fused_computation.12 | convolution fusion | flops 704708608 | bytes 2818048 | tf_op jit(solution)/shard_map/dot_general | solution.py:76
  371.2 4.1 %collective-permute-start.2 = (bf16[1,512,1024]{1,2,0:T(8,128)(2,1)S(1)}, bf16[1,512,1024]{1,2,0:T(8,128)(2,1)S(1)}, u32[]{:S(2)}, u32[]{:S(2)}) collective-permute-start(bf16[1,512,1024]{1,2,0:T(8,128)(2,1)S(1)} %fusion.7), channel_id=1, source_target_pairs={{0,16},{16,32},{32,48},{48,64},{64,80},{80,96},{96,112},{112,128},... | collective-permute-start | bytes 3145736 | tf_op jit(solution)/shard_map/ppermute | solution.py:72
  376.3 10.8 %collective-permute-done.2 = bf16[1,512,1024]{1,2,0:T(8,128)(2,1)S(1)} collective-permute-done((bf16[1,512,1024]{1,2,0:T(8,128)(2,1)S(1)}, bf16[1,512,1024]{1,2,0:T(8,128)(2,1)S(1)}, u32[]{:S(2)}, u32[]{:S(2)}) %collective-permute-start.2) | collective-permute-done | bytes 1048608 | tf_op jit(solution)/shard_map/ppermute | solution.py:72
  (201 shorter events, 81.8 us)
Async XLA Ops:
  7.2 17.9 %copy-start.14 = (bf16[1,512,1024]{2,1,0:T(8,128)(2,1)S(1)}, bf16[1,512,1024]{2,1,0:T(8,128)(2,1)}, u32[]{:S(2)}) copy-start(bf16[1,512,1024]{2,1,0:T(8,128)(2,1)} %param.5) | copy-start | bytes 3145732
  7.2 11.0 %copy-start.40 = (s32[1,8,4]{1,2,0:T(4,128)S(1)}, s32[1,8,4]{1,2,0:T(4,128)}, u32[]{:S(2)}) copy-start(s32[1,8,4]{1,2,0:T(4,128)} %param.8) | copy-start | bytes 388
  7.2 11.3 %copy-start.28 = (bf16[1,512,256]{2,1,0:T(8,128)(2,1)S(1)}, bf16[1,512,256]{2,1,0:T(8,128)(2,1)}, u32[]{:S(2)}) copy-start(bf16[1,512,256]{2,1,0:T(8,128)(2,1)} %param.7) | copy-start | bytes 786436
  7.2 173.0 %all-reduce.2.cloned.1.call-start = ((), (), s32[]{:S(2)}) async-start(), calls=%async_computation | async-start | bytes 8388608 | tf_op jit(solution)/shard_map/psum | solution.py:101
  8.6 14.2 %collective-permute-start = (bf16[256,1024]{1,0:T(8,128)(2,1)S(1)}, bf16[256,1024]{1,0:T(8,128)(2,1)S(1)}, u32[]{:S(2)}, u32[]{:S(2)}) collective-permute-start(bf16[256,1024]{1,0:T(8,128)(2,1)S(1)} %get-tuple-element.38), channel_id=1, source_target_pairs={{0,1},{1,2},{2,3},{3,4},{4,5},{5,6},{6,7},{7,8},{8,9},{9,10},{10,1... | collective-permute-start | bytes 1572872 | tf_op jit(solution)/shard_map/ppermute | solution.py:61
  12.6 11.7 %collective-permute-start.1 = (bf16[256,1024]{1,0:T(8,128)(2,1)S(1)}, bf16[256,1024]{1,0:T(8,128)(2,1)S(1)}, u32[]{:S(2)}, u32[]{:S(2)}) collective-permute-start(bf16[256,1024]{1,0:T(8,128)(2,1)S(1)} %get-tuple-element.39), channel_id=1, source_target_pairs={{1,0},{2,1},{3,2},{4,3},{5,4},{6,5},{7,6},{8,7},{9,8},{10,9},{11,1... | collective-permute-start | bytes 1572872 | tf_op jit(solution)/shard_map/ppermute | solution.py:64
  32.7 6.3 %copy-start.21 = (bf16[8,1024,64]{1,2,0:T(8,128)(2,1)}, bf16[8,1024,64]{1,2,0:T(8,128)(2,1)S(1)}, u32[]{:S(2)}) copy-start(bf16[8,1024,64]{1,2,0:T(8,128)(2,1)S(1)} %bitcast_convert_fusion) | copy-start | bytes 3145732
  204.2 13.2 %copy-start.18 = (f32[896,128]{0,1:T(8,128)}, f32[896,128]{0,1:T(8,128)S(1)}, u32[]{:S(2)}) copy-start(f32[896,128]{0,1:T(8,128)S(1)} %convolution_subtract_fusion) | copy-start | bytes 1376260
  204.2 18.1 %copy-start.37 = (f32[128,128]{1,0:T(8,128)S(1)}, f32[128,128]{1,0:T(8,128)}, u32[]{:S(2)}) copy-start(f32[128,128]{1,0:T(8,128)} %get-tuple-element.26) | copy-start | bytes 196612
  204.2 18.2 %copy-start.32 = (f32[128,128]{1,0:T(8,128)S(1)}, f32[128,128]{1,0:T(8,128)}, u32[]{:S(2)}) copy-start(f32[128,128]{1,0:T(8,128)} %get-tuple-element.18) | copy-start | bytes 196612
  220.3 5.6 %copy-start.38 = (f32[128,128]{1,0:T(8,128)S(1)}, f32[128,128]{1,0:T(8,128)}, u32[]{:S(2)}) copy-start(f32[128,128]{1,0:T(8,128)} %get-tuple-element.27) | copy-start | bytes 196612
  220.3 5.9 %copy-start.4 = (f32[768,128]{0,1:T(8,128)S(1)}, f32[768,128]{0,1:T(8,128)}, u32[]{:S(2)}) copy-start(f32[768,128]{0,1:T(8,128)} %slice.259) | copy-start | bytes 1179652
  228.9 23.0 %copy-start.1 = (f32[512,128]{0,1:T(8,128)}, f32[512,128]{0,1:T(8,128)S(1)}, u32[]{:S(2)}) copy-start(f32[512,128]{0,1:T(8,128)S(1)} %get-tuple-element.60) | copy-start | bytes 786436
  277.4 20.9 %copy-start.23 = (f32[512,128]{0,1:T(8,128)S(1)}, f32[512,128]{0,1:T(8,128)}, u32[]{:S(2)}) copy-start(f32[512,128]{0,1:T(8,128)} %copy-done.22) | copy-start | bytes 786436
  291.4 6.9 %copy-start.29 = (f32[128,128]{1,0:T(8,128)S(1)}, f32[128,128]{1,0:T(8,128)}, u32[]{:S(2)}) copy-start(f32[128,128]{1,0:T(8,128)} %get-tuple-element.22) | copy-start | bytes 196612
  319.1 32.9 %copy-start.25 = (f32[512,128]{1,0:T(8,128)S(1)}, f32[512,128]{1,0:T(8,128)}, u32[]{:S(2)}) copy-start(f32[512,128]{1,0:T(8,128)} %convolution_subtract_fusion.10) | copy-start | bytes 786436
  321.2 31.8 %copy-start.3 = (f32[512,128]{0,1:T(8,128)S(1)}, f32[512,128]{0,1:T(8,128)}, u32[]{:S(2)}) copy-start(f32[512,128]{0,1:T(8,128)} %copy-done.1) | copy-start | bytes 786436
  334.9 19.1 %copy-start.13 = (f32[512,128]{0,1:T(8,128)S(1)}, f32[512,128]{0,1:T(8,128)}, u32[]{:S(2)}) copy-start(f32[512,128]{0,1:T(8,128)} %copy-done.11) | copy-start | bytes 786436
  338.7 16.4 %copy-start.17 = (f32[512,128]{0,1:T(8,128)S(1)}, f32[512,128]{0,1:T(8,128)}, u32[]{:S(2)}) copy-start(f32[512,128]{0,1:T(8,128)} %copy-done.16) | copy-start | bytes 786436
  366.5 8.8 %copy-start.35 = (f32[128,128]{1,0:T(8,128)S(1)}, f32[128,128]{1,0:T(8,128)}, u32[]{:S(2)}) copy-start(f32[128,128]{1,0:T(8,128)} %get-tuple-element.32) | copy-start | bytes 196612
  366.5 8.9 %copy-start.36 = (f32[128,128]{1,0:T(8,128)S(1)}, f32[128,128]{1,0:T(8,128)}, u32[]{:S(2)}) copy-start(f32[128,128]{1,0:T(8,128)} %get-tuple-element.33) | copy-start | bytes 196612
  366.6 9.1 %copy-start.41 = (f32[1,1024]{1,0:T(1,128)S(1)}, f32[1,1024]{1,0:T(1,128)}, u32[]{:S(2)}) copy-start(f32[1,1024]{1,0:T(1,128)} %param.9) | copy-start | bytes 12292
  366.6 20.4 %copy-start.10 = (bf16[512,1024]{0,1:T(8,128)(2,1)S(1)}, bf16[512,1024]{0,1:T(8,128)(2,1)}, u32[]{:S(2)}) copy-start(bf16[512,1024]{0,1:T(8,128)(2,1)} %copy.41) | copy-start | bytes 3145732
  371.2 15.8 %collective-permute-start.2 = (bf16[1,512,1024]{1,2,0:T(8,128)(2,1)S(1)}, bf16[1,512,1024]{1,2,0:T(8,128)(2,1)S(1)}, u32[]{:S(2)}, u32[]{:S(2)}) collective-permute-start(bf16[1,512,1024]{1,2,0:T(8,128)(2,1)S(1)} %fusion.7), channel_id=1, source_target_pairs={{0,16},{16,32},{32,48},{48,64},{64,80},{80,96},{96,112},{112,128},... | collective-permute-start | bytes 3145736 | tf_op jit(solution)/shard_map/ppermute | solution.py:72
  (22 other events, 84.1 us)
Sparse Core Ops, SparseCore 0:
  36.2 143.8 all-reduce.1

commit v2 on v1

--- a/solution.py
+++ b/solution.py
@@ -72,6 +72,47 @@
     return lax.ppermute(array, axis, pairs)
 
 
+GROUP = 4
+
+
+def ring_pairs(count, stride, by):
+    pairs = []
+    for i in range(count):
+        place = (i // stride) % GROUP
+        pairs.append((i, i + ((place + by) % GROUP - place) * stride))
+    return pairs
+
+
+def scatter_sum(data, stride):
+    count = lax.axis_size("row")
+    place = (lax.axis_index("row") // stride) % GROUP
+    chunks = data.reshape(GROUP, data.shape[0] // GROUP, data.shape[1])
+    total = lax.dynamic_index_in_dim(chunks, place, 0, keepdims=False)
+    for by in range(1, GROUP):
+        sent = lax.dynamic_index_in_dim(chunks, (place + by) % GROUP, 0, keepdims=False)
+        total = total + lax.ppermute(sent, "row", ring_pairs(count, stride, by))
+    return total
+
+
+def gather_all(piece, stride):
+    count = lax.axis_size("row")
+    place = (lax.axis_index("row") // stride) % GROUP
+    parts = [piece] + [
+        lax.ppermute(piece, "row", ring_pairs(count, stride, by)) for by in range(1, GROUP)
+    ]
+    order = [parts[0]] + parts[:0:-1]
+    doubled = jnp.stack(order + order)
+    picked = lax.dynamic_slice_in_dim(doubled, (GROUP - place) % GROUP, GROUP, axis=0)
+    return picked.reshape(GROUP * piece.shape[0], piece.shape[1])
+
+
+def row_sum(data):
+    inner = scatter_sum(data, 1)
+    both = scatter_sum(inner, GROUP)
+    inner = gather_all(both, GROUP)
+    return gather_all(inner, 1)
+
+
 def times_t(a, b):
     return lax.dot_general(
         a, b, (((1,), (1,)), ((), ())), precision=HIGHEST, preferred_element_type=jnp.float32
@@ -95,20 +136,27 @@
     wide_rows = propagated.astype(jnp.float32)
     scale = 1.0 / (row_count * lax.axis_size("row"))
 
-    partial_value = lax.dot_general(
-        propagated, propagated, (((0,), (0,)), ((), ())), preferred_element_type=jnp.float32
-    )
-    gram_matrix = lax.psum(partial_value, "row") * scale
-
     width = PANEL
     panels = col_count // width
     eye = jnp.eye(width, dtype=jnp.float32)
+    parts = [
+        lax.dot_general(
+            propagated[:, k * width:],
+            propagated[:, k * width:(k + 1) * width],
+            (((0,), (0,)), ((), ())),
+            preferred_element_type=jnp.float32,
+        )
+        for k in range(panels)
+    ]
+    packed = row_sum(jnp.concatenate(parts, axis=0)) * scale
     columns = []
     solved = []
     logs = []
+    start = 0
     for k in range(panels):
         low = k * width
-        panel = gram_matrix[low:, low:low + width]
+        panel = packed[start:start + col_count - low]
+        start += col_count - low
         if k:
             left = jnp.concatenate(
                 [column[low - j * width:] for j, column in enumerate(columns)], axis=1

time: 400 us -> 367 us (0.917)
  the two profiles are of different devices: /device:TPU:1 before, /device:TPU:384 now
where the time goes in v2:
time: 367 us; the launch traced here: 359 us
  Pallas kernels  99.2 us (27%)
  waiting for transfers between devices  76.1 us (21%)
  matrix products  56.2 us (15%)
  local copies, waits for them, and re-layouts  55.4 us (15%)
  starting transfers between devices  52.6 us (14%)
  other arithmetic  17.7 us (5%)
    pallas_call x8, Pallas kernels, chol_inv(): pl.pallas_call(_chol_inv_kernel, out_shape=(jax.ShapeDtypeStruct((n, n),...  99.2 us
    dot_general x29, matrix products, times_t(): lax.dot_general(a, b, (((1,), (1,)), ((), ())), precision=HIGHEST, prefer...  50 us
    unnamed x149, local copies, waits for them, and re-layouts  32.7 us
    ppermute x6, waiting for transfers between devices, gather_all(): lax.ppermute(piece, 'row', ring_pairs(count, stride, by))  26 us
    ppermute x6, waiting for transfers between devices, scatter_sum(): total = total + lax.ppermute(sent, 'row', ring_pairs(count, stride, by))  26 us
    ppermute x6, starting transfers between devices, scatter_sum(): total = total + lax.ppermute(sent, 'row', ring_pairs(count, stride, by))  20.9 us
    ppermute x6, starting transfers between devices, gather_all(): lax.ppermute(piece, 'row', ring_pairs(count, stride, by))  20.6 us
    ppermute x1, waiting for transfers between devices, shifted(): return lax.ppermute(array, axis, pairs)  14.4 us
  transfers between devices with their start and end apart: 15, of which 11 were waited for; matrix products, arithmetic and copies ran while one was open for 2% of the time, Pallas kernels for 0%

profile of v2, /device:TPU:384, one launch (start us, length us, event | category | flops | bytes accessed | tf_op | source)
XLA Modules:
  0.0 359.3 jit_solution(2028475870248562841)
XLA Ops:
  5.5 5.7 %collective-permute-start.1 = (bf16[256,1024]{1,0:T(8,128)(2,1)S(1)}, bf16[256,1024]{1,0:T(8,128)(2,1)S(1)}, u32[]{:S(2)}, u32[]{:S(2)}) collective-permute-start(bf16[256,1024]{1,0:T(8,128)(2,1)S(1)} %get-tuple-element.46), channel_id=1, source_target_pairs={{1,0},{2,1},{3,2},{4,3},{5,4},{6,5},{7,6},{8,7},{9,8},{10,9},{11,1... | collective-permute-start | bytes 1572872 | tf_op jit(solution)/shard_map/ppermute | solution.py:64
  12.7 8.4 %collective-permute-done = bf16[256,1024]{1,0:T(8,128)(2,1)S(1)} collective-permute-done((bf16[256,1024]{1,0:T(8,128)(2,1)S(1)}, bf16[256,1024]{1,0:T(8,128)(2,1)S(1)}, u32[]{:S(2)}, u32[]{:S(2)}) %collective-permute-start) | collective-permute-done | bytes 524320 | tf_op jit(solution)/shard_map/ppermute | solution.py:61
  36.8 5.0 %collective-permute-start.4 = (f32[1152,128]{1,0:T(8,128)}, f32[1152,128]{1,0:T(8,128)}, u32[]{:S(2)}, u32[]{:S(2)}) collective-permute-start(f32[1152,128]{1,0:T(8,128)} %get-tuple-element.43), channel_id=1, source_target_pairs={{0,3},{1,0},{2,1},{3,2},{4,7},{5,4},{6,5},{7,6},{8,11},{9,8},{10,9... | collective-permute-start | bytes 1769480 | tf_op jit(solution)/shard_map/ppermute | solution.py:93
  45.3 8.2 %collective-permute-done.2 = f32[1152,128]{1,0:T(8,128)} collective-permute-done((f32[1152,128]{1,0:T(8,128)}, f32[1152,128]{1,0:T(8,128)}, u32[]{:S(2)}, u32[]{:S(2)}) %collective-permute-start.2) | collective-permute-done | bytes 589856 | tf_op jit(solution)/shard_map/ppermute | solution.py:93
  53.5 12.7 %collective-permute-done.4 = f32[1152,128]{1,0:T(8,128)} collective-permute-done((f32[1152,128]{1,0:T(8,128)}, f32[1152,128]{1,0:T(8,128)}, u32[]{:S(2)}, u32[]{:S(2)}) %collective-permute-start.4) | collective-permute-done | bytes 589856 | tf_op jit(solution)/shard_map/ppermute | solution.py:93
  72.1 3.7 %collective-permute-start.7 = (f32[288,128]{1,0:T(8,128)S(1)}, f32[288,128]{1,0:T(8,128)S(1)}, u32[]{:S(2)}, u32[]{:S(2)}) collective-permute-start(f32[288,128]{1,0:T(8,128)S(1)} %get-tuple-element.48), channel_id=1, source_target_pairs={{0,12},{1,13},{2,14},{3,15},{4,0},{5,1},{6,2},{7,3},{8,4},{9,5},{1... | collective-permute-start | bytes 442376 | tf_op jit(solution)/shard_map/ppermute | solution.py:93
  80.0 4.3 %collective-permute-done.6 = f32[288,128]{1,0:T(8,128)S(1)} collective-permute-done((f32[288,128]{1,0:T(8,128)S(1)}, f32[288,128]{1,0:T(8,128)S(1)}, u32[]{:S(2)}, u32[]{:S(2)}) %collective-permute-start.6) | collective-permute-done | bytes 147488 | tf_op jit(solution)/shard_map/ppermute | solution.py:93
  85.9 3.9 %collective-permute-start.8 = (f32[288,128]{1,0:T(8,128)S(1)}, f32[288,128]{1,0:T(8,128)S(1)}, u32[]{:S(2)}, u32[]{:S(2)}) collective-permute-start(f32[288,128]{1,0:T(8,128)S(1)} %get-tuple-element.39), channel_id=1, source_target_pairs={{0,12},{1,13},{2,14},{3,15},{4,0},{5,1},{6,2},{7,3},{8,4},{9,5},{1... | collective-permute-start | bytes 442376 | tf_op jit(solution)/shard_map/ppermute | solution.py:101
  95.9 4.5 %collective-permute-done.9 = f32[288,128]{1,0:T(8,128)S(1)} collective-permute-done((f32[288,128]{1,0:T(8,128)S(1)}, f32[288,128]{1,0:T(8,128)S(1)}, u32[]{:S(2)}, u32[]{:S(2)}) %collective-permute-start.9) | collective-permute-done | bytes 147488 | tf_op jit(solution)/shard_map/ppermute | solution.py:101
  105.5 5.6 %collective-permute-start.11 = (f32[1152,128]{1,0:T(8,128)S(1)}, f32[1152,128]{1,0:T(8,128)S(1)}, u32[]{:S(2)}, u32[]{:S(2)}) collective-permute-start(f32[1152,128]{1,0:T(8,128)S(1)} %bitcast.222), channel_id=1, source_target_pairs={{0,3},{1,0},{2,1},{3,2},{4,7},{5,4},{6,5},{7,6},{8,11},{9,8},{10,9... | collective-permute-start | bytes 1769480 | tf_op jit(solution)/shard_map/ppermute | solution.py:101
  116.1 3.8 %collective-permute-start.12 = (f32[1152,128]{1,0:T(8,128)S(1)}, f32[1152,128]{1,0:T(8,128)S(1)}, u32[]{:S(2)}, u32[]{:S(2)}) collective-permute-start(f32[1152,128]{1,0:T(8,128)S(1)} %bitcast.224), channel_id=1, source_target_pairs={{0,2},{1,3},{2,0},{3,1},{4,6},{5,7},{6,4},{7,5},{8,10},{9,11},{10,... | collective-permute-start | bytes 1769480 | tf_op jit(solution)/shard_map/ppermute | solution.py:101
  120.0 13.3 %collective-permute-done.11 = f32[1152,128]{1,0:T(8,128)S(1)} collective-permute-done((f32[1152,128]{1,0:T(8,128)S(1)}, f32[1152,128]{1,0:T(8,128)S(1)}, u32[]{:S(2)}, u32[]{:S(2)}) %collective-permute-start.11) | collective-permute-done | bytes 589856 | tf_op jit(solution)/shard_map/ppermute | solution.py:101
  133.3 6.9 %collective-permute-done.12 = f32[1152,128]{1,0:T(8,128)S(1)} collective-permute-done((f32[1152,128]{1,0:T(8,128)S(1)}, f32[1152,128]{1,0:T(8,128)S(1)}, u32[]{:S(2)}, u32[]{:S(2)}) %collective-permute-start.12) | collective-permute-done | bytes 589856 | tf_op jit(solution)/shard_map/ppermute | solution.py:101
  145.7 12.3 %shard_map.68 = (f32[128,128]{1,0:T(8,128)}, f32[128,128]{1,0:T(8,128)}) custom-call(f32[128,128]{1,0:T(8,128)} %copy.57.a_ref), custom_call_target="tpu_custom_call" | custom-call | tf_op jit(solution)/shard_map/pallas_call | solution.py:41
  167.8 12.3 %shard_map.69 = (f32[128,128]{1,0:T(8,128)}, f32[128,128]{1,0:T(8,128)}) custom-call(f32[128,128]{1,0:T(8,128)} %copy.61.a_ref), custom_call_target="tpu_custom_call" | custom-call | tf_op jit(solution)/shard_map/pallas_call | solution.py:41
  202.7 12.3 %shard_map.70 = (f32[128,128]{1,0:T(8,128)}, f32[128,128]{1,0:T(8,128)}) custom-call(f32[128,128]{1,0:T(8,128)} %copy.65.a_ref), custom_call_target="tpu_custom_call" | custom-call | tf_op jit(solution)/shard_map/pallas_call | solution.py:41
  226.3 12.5 %shard_map.71 = (f32[128,128]{1,0:T(8,128)}, f32[128,128]{1,0:T(8,128)}) custom-call(f32[128,128]{1,0:T(8,128)} %copy.69.a_ref), custom_call_target="tpu_custom_call" | custom-call | tf_op jit(solution)/shard_map/pallas_call | solution.py:41
  250.2 12.3 %shard_map.72 = (f32[128,128]{1,0:T(8,128)}, f32[128,128]{1,0:T(8,128)}) custom-call(f32[128,128]{1,0:T(8,128)} %copy.73.a_ref), custom_call_target="tpu_custom_call" | custom-call | tf_op jit(solution)/shard_map/pallas_call | solution.py:41
  274.8 12.7 %shard_map.73 = (f32[128,128]{1,0:T(8,128)}, f32[128,128]{1,0:T(8,128)}) custom-call(f32[128,128]{1,0:T(8,128)} %copy.77.a_ref), custom_call_target="tpu_custom_call" | custom-call | tf_op jit(solution)/shard_map/pallas_call | solution.py:41
  293.6 12.3 %shard_map.74 = (f32[128,128]{1,0:T(8,128)}, f32[128,128]{1,0:T(8,128)}) custom-call(f32[128,128]{1,0:T(8,128)} %fusion.84.a_ref), custom_call_target="tpu_custom_call" | custom-call | tf_op jit(solution)/shard_map/pallas_call | solution.py:41
  308.8 12.5 %shard_map.75 = (f32[128,128]{1,0:T(8,128)}, f32[128,128]{1,0:T(8,128)}) custom-call(f32[128,128]{1,0:T(8,128)} %broadcast_multiply_fusion.a_ref), custom_call_target="tpu_custom_call" | custom-call | tf_op jit(solution)/shard_map/pallas_call | solution.py:41
  327.3 3.8 %convolution_subtract_fusion.4 = f32[512,128]{1,0:T(8,128)S(1)} fusion(f32[512,640]{0,1:T(8,128)} %get-tuple-element.54, f32[384,640]{0,1:T(8,128)} %get-tuple-element.77, f32[512,1024]{1,0:T(8,128)S(1)} %copy-done), kind=kOutput, calls=%fused_computation.18 | convolution fusion | flops 503382016 | bytes 2162688 | tf_op jit(solution)/shard_map/dot_general | solution.py:117
  332.3 4.0 %convolution_subtract_fusion.7 = f32[512,128]{1,0:T(8,128)S(1)} fusion(f32[512,768]{0,1:T(8,128)} %get-tuple-element.51, f32[256,768]{0,1:T(8,128)S(1)} %copy-done.17, f32[512,1024]{1,0:T(8,128)S(1)} %copy-done), kind=kOutput, calls=%fused_computation.21 | convolution fusion | flops 604045312 | bytes 2490368 | tf_op jit(solution)/shard_map/dot_general | solution.py:117
  343.3 14.4 %collective-permute-done.14 = bf16[1,512,1024]{1,2,0:T(8,128)(2,1)S(1)} collective-permute-done((bf16[1,512,1024]{1,2,0:T(8,128)(2,1)S(1)}, bf16[1,512,1024]{1,2,0:T(8,128)(2,1)S(1)}, u32[]{:S(2)}, u32[]{:S(2)}) %collective-permute-start.14) | collective-permute-done | bytes 1048608 | tf_op jit(solution)/shard_map/ppermute | solution.py:72
  (276 shorter events, 149.7 us)
Async XLA Ops:
  0.6 22.4 %copy-start.16 = (bf16[1,512,1024]{2,1,0:T(8,128)(2,1)S(1)}, bf16[1,512,1024]{2,1,0:T(8,128)(2,1)}, u32[]{:S(2)}) copy-start(bf16[1,512,1024]{2,1,0:T(8,128)(2,1)} %param.5) | copy-start | bytes 3145732
  2.0 19.0 %collective-permute-start = (bf16[256,1024]{1,0:T(8,128)(2,1)S(1)}, bf16[256,1024]{1,0:T(8,128)(2,1)S(1)}, u32[]{:S(2)}, u32[]{:S(2)}) collective-permute-start(bf16[256,1024]{1,0:T(8,128)(2,1)S(1)} %get-tuple-element.45), channel_id=1, source_target_pairs={{0,1},{1,2},{2,3},{3,4},{4,5},{5,6},{6,7},{7,8},{8,9},{9,10},{10,1... | collective-permute-start | bytes 1572872 | tf_op jit(solution)/shard_map/ppermute | solution.py:61
  5.5 16.7 %collective-permute-start.1 = (bf16[256,1024]{1,0:T(8,128)(2,1)S(1)}, bf16[256,1024]{1,0:T(8,128)(2,1)S(1)}, u32[]{:S(2)}, u32[]{:S(2)}) collective-permute-start(bf16[256,1024]{1,0:T(8,128)(2,1)S(1)} %get-tuple-element.46), channel_id=1, source_target_pairs={{1,0},{2,1},{3,2},{4,3},{5,4},{6,5},{7,6},{8,7},{9,8},{10,9},{11,1... | collective-permute-start | bytes 1572872 | tf_op jit(solution)/shard_map/ppermute | solution.py:64
  30.6 81.9 %copy-start.5 = (bf16[8,1024,64]{1,2,0:T(8,128)(2,1)}, bf16[8,1024,64]{1,2,0:T(8,128)(2,1)S(1)}, u32[]{:S(2)}) copy-start(bf16[8,1024,64]{1,2,0:T(8,128)(2,1)S(1)} %bitcast_convert_fusion) | copy-start | bytes 3145732
  34.8 18.7 %collective-permute-start.2 = (f32[1152,128]{1,0:T(8,128)}, f32[1152,128]{1,0:T(8,128)}, u32[]{:S(2)}, u32[]{:S(2)}) collective-permute-start(f32[1152,128]{1,0:T(8,128)} %get-tuple-element.42), channel_id=1, source_target_pairs={{0,1},{1,2},{2,3},{3,0},{4,5},{5,6},{6,7},{7,4},{8,9},{9,10},{10,1... | collective-permute-start | bytes 1769480 | tf_op jit(solution)/shard_map/ppermute | solution.py:93
  36.8 29.4 %collective-permute-start.4 = (f32[1152,128]{1,0:T(8,128)}, f32[1152,128]{1,0:T(8,128)}, u32[]{:S(2)}, u32[]{:S(2)}) collective-permute-start(f32[1152,128]{1,0:T(8,128)} %get-tuple-element.43), channel_id=1, source_target_pairs={{0,3},{1,0},{2,1},{3,2},{4,7},{5,4},{6,5},{7,6},{8,11},{9,8},{10,9... | collective-permute-start | bytes 1769480 | tf_op jit(solution)/shard_map/ppermute | solution.py:93
  41.9 24.4 %collective-permute-start.3 = (f32[1152,128]{1,0:T(8,128)}, f32[1152,128]{1,0:T(8,128)}, u32[]{:S(2)}, u32[]{:S(2)}) collective-permute-start(f32[1152,128]{1,0:T(8,128)} %get-tuple-element.44), channel_id=1, source_target_pairs={{0,2},{1,3},{2,0},{3,1},{4,6},{5,7},{6,4},{7,5},{8,10},{9,11},{10,... | collective-permute-start | bytes 1769480 | tf_op jit(solution)/shard_map/ppermute | solution.py:93
  68.7 10.5 %collective-permute-start.5 = (f32[288,128]{1,0:T(8,128)S(1)}, f32[288,128]{1,0:T(8,128)S(1)}, u32[]{:S(2)}, u32[]{:S(2)}) collective-permute-start(f32[288,128]{1,0:T(8,128)S(1)} %get-tuple-element.47), channel_id=1, source_target_pairs={{0,4},{1,5},{2,6},{3,7},{4,8},{5,9},{6,10},{7,11},{8,12},{9,13},{1... | collective-permute-start | bytes 442376 | tf_op jit(solution)/shard_map/ppermute | solution.py:93
  72.1 8.0 %collective-permute-start.7 = (f32[288,128]{1,0:T(8,128)S(1)}, f32[288,128]{1,0:T(8,128)S(1)}, u32[]{:S(2)}, u32[]{:S(2)}) collective-permute-start(f32[288,128]{1,0:T(8,128)S(1)} %get-tuple-element.48), channel_id=1, source_target_pairs={{0,12},{1,13},{2,14},{3,15},{4,0},{5,1},{6,2},{7,3},{8,4},{9,5},{1... | collective-permute-start | bytes 442376 | tf_op jit(solution)/shard_map/ppermute | solution.py:93
  75.8 8.5 %collective-permute-start.6 = (f32[288,128]{1,0:T(8,128)S(1)}, f32[288,128]{1,0:T(8,128)S(1)}, u32[]{:S(2)}, u32[]{:S(2)}) collective-permute-start(f32[288,128]{1,0:T(8,128)S(1)} %get-tuple-element.49), channel_id=1, source_target_pairs={{0,8},{1,9},{2,10},{3,11},{4,12},{5,13},{6,14},{7,15},{8,0},{9,1},... | collective-permute-start | bytes 442376 | tf_op jit(solution)/shard_map/ppermute | solution.py:93
  79.2 31.9 %copy-start.26 = (bf16[512,1024]{1,0:T(8,128)(2,1)S(1)}, bf16[512,1024]{1,0:T(8,128)(2,1)}, u32[]{:S(2)}) copy-start(bf16[512,1024]{1,0:T(8,128)(2,1)} %param.6) | copy-start | bytes 3145732
  85.9 9.3 %collective-permute-start.8 = (f32[288,128]{1,0:T(8,128)S(1)}, f32[288,128]{1,0:T(8,128)S(1)}, u32[]{:S(2)}, u32[]{:S(2)}) collective-permute-start(f32[288,128]{1,0:T(8,128)S(1)} %get-tuple-element.39), channel_id=1, source_target_pairs={{0,12},{1,13},{2,14},{3,15},{4,0},{5,1},{6,2},{7,3},{8,4},{9,5},{1... | collective-permute-start | bytes 442376 | tf_op jit(solution)/shard_map/ppermute | solution.py:101
  89.9 11.1 %collective-permute-start.10 = (f32[288,128]{1,0:T(8,128)S(1)}, f32[288,128]{1,0:T(8,128)S(1)}, u32[]{:S(2)}, u32[]{:S(2)}) collective-permute-start(f32[288,128]{1,0:T(8,128)S(1)} %get-tuple-element.39), channel_id=1, source_target_pairs={{0,4},{1,5},{2,6},{3,7},{4,8},{5,9},{6,10},{7,11},{8,12},{9,13},{1... | collective-permute-start | bytes 442376 | tf_op jit(solution)/shard_map/ppermute | solution.py:101
  91.8 8.5 %collective-permute-start.9 = (f32[288,128]{1,0:T(8,128)S(1)}, f32[288,128]{1,0:T(8,128)S(1)}, u32[]{:S(2)}, u32[]{:S(2)}) collective-permute-start(f32[288,128]{1,0:T(8,128)S(1)} %get-tuple-element.39), channel_id=1, source_target_pairs={{0,8},{1,9},{2,10},{3,11},{4,12},{5,13},{6,14},{7,15},{8,0},{9,1},... | collective-permute-start | bytes 442376 | tf_op jit(solution)/shard_map/ppermute | solution.py:101
  105.5 27.8 %collective-permute-start.11 = (f32[1152,128]{1,0:T(8,128)S(1)}, f32[1152,128]{1,0:T(8,128)S(1)}, u32[]{:S(2)}, u32[]{:S(2)}) collective-permute-start(f32[1152,128]{1,0:T(8,128)S(1)} %bitcast.222), channel_id=1, source_target_pairs={{0,3},{1,0},{2,1},{3,2},{4,7},{5,4},{6,5},{7,6},{8,11},{9,8},{10,9... | collective-permute-start | bytes 1769480 | tf_op jit(solution)/shard_map/ppermute | solution.py:101
  114.1 27.5 %collective-permute-start.13 = (f32[1152,128]{1,0:T(8,128)S(1)}, f32[1152,128]{1,0:T(8,128)S(1)}, u32[]{:S(2)}, u32[]{:S(2)}) collective-permute-start(f32[1152,128]{1,0:T(8,128)S(1)} %bitcast.223), channel_id=1, source_target_pairs={{0,1},{1,2},{2,3},{3,0},{4,5},{5,6},{6,7},{7,4},{8,9},{9,10},{10,1... | collective-permute-start | bytes 1769480 | tf_op jit(solution)/shard_map/ppermute | solution.py:101
  116.1 24.2 %collective-permute-start.12 = (f32[1152,128]{1,0:T(8,128)S(1)}, f32[1152,128]{1,0:T(8,128)S(1)}, u32[]{:S(2)}, u32[]{:S(2)}) collective-permute-start(f32[1152,128]{1,0:T(8,128)S(1)} %bitcast.224), channel_id=1, source_target_pairs={{0,2},{1,3},{2,0},{3,1},{4,6},{5,7},{6,4},{7,5},{8,10},{9,11},{10,... | collective-permute-start | bytes 1769480 | tf_op jit(solution)/shard_map/ppermute | solution.py:101
  199.3 39.5 %copy-start.1 = (f32[512,128]{0,1:T(8,128)}, f32[512,128]{0,1:T(8,128)S(1)}, u32[]{:S(2)}) copy-start(f32[512,128]{0,1:T(8,128)S(1)} %get-tuple-element.70) | copy-start | bytes 786436
  269.3 21.5 %copy-start.30 = (f32[256,128]{0,1:T(8,128)S(1)}, f32[256,128]{0,1:T(8,128)}, u32[]{:S(2)}) copy-start(f32[256,128]{0,1:T(8,128)} %copy.100) | copy-start | bytes 393220
  273.9 33.1 %copy-start.34 = (f32[128,128]{0,1:T(8,128)S(1)}, f32[128,128]{0,1:T(8,128)}, u32[]{:S(2)}) copy-start(f32[128,128]{0,1:T(8,128)} %copy.101) | copy-start | bytes 196612
  290.8 32.5 %copy-start.3 = (f32[512,128]{0,1:T(8,128)S(1)}, f32[512,128]{0,1:T(8,128)}, u32[]{:S(2)}) copy-start(f32[512,128]{0,1:T(8,128)} %copy-done.1) | copy-start | bytes 786436
  292.9 31.4 %copy-start.15 = (f32[512,128]{0,1:T(8,128)S(1)}, f32[512,128]{0,1:T(8,128)}, u32[]{:S(2)}) copy-start(f32[512,128]{0,1:T(8,128)} %copy-done.13) | copy-start | bytes 786436
  336.8 20.9 %copy-start.12 = (bf16[512,1024]{0,1:T(8,128)(2,1)S(1)}, bf16[512,1024]{0,1:T(8,128)(2,1)}, u32[]{:S(2)}) copy-start(bf16[512,1024]{0,1:T(8,128)(2,1)} %copy.50) | copy-start | bytes 3145732
  340.4 17.3 %collective-permute-start.14 = (bf16[1,512,1024]{1,2,0:T(8,128)(2,1)S(1)}, bf16[1,512,1024]{1,2,0:T(8,128)(2,1)S(1)}, u32[]{:S(2)}, u32[]{:S(2)}) collective-permute-start(bf16[1,512,1024]{1,2,0:T(8,128)(2,1)S(1)} %fusion.7), channel_id=1, source_target_pairs={{0,16},{16,32},{32,48},{48,64},{64,80},{80,96},{96,112},{112,128},... | collective-permute-start | bytes 3145736 | tf_op jit(solution)/shard_map/ppermute | solution.py:72
  (40 other events, 242.5 us)

commit v3 on v2

--- a/solution.py
+++ b/solution.py
@@ -107,10 +107,14 @@
 
 
 def row_sum(data):
-    inner = scatter_sum(data, 1)
-    both = scatter_sum(inner, GROUP)
-    inner = gather_all(both, GROUP)
-    return gather_all(inner, 1)
+    count = lax.axis_size("row")
+    chunks = data.reshape(count, data.shape[0] // count, data.shape[1])
+    received = lax.all_to_all(chunks, "row", 0, 0)
+    total = received[0]
+    for j in range(1, count):
+        total = total + received[j]
+    spread = jnp.broadcast_to(total[None], chunks.shape)
+    return lax.all_to_all(spread, "row", 0, 0).reshape(data.shape)
 
 
 def times_t(a, b):

time: 367 us -> 332 us (0.905)
  the two profiles are of different devices: /device:TPU:384 before, /device:TPU:256 now
where the time goes in v3:
time: 332 us; the launch traced here: 326 us
  Pallas kernels  99.1 us (30%)
  matrix products  56.3 us (17%)
  waiting for transfers between devices  51.1 us (15%)
  local copies, waits for them, and re-layouts  44.6 us (13%)
  blocking collectives  37 us (11%)
  other arithmetic  20.2 us (6%)
  starting transfers between devices  15.7 us (5%)
    pallas_call x8, Pallas kernels, chol_inv(): pl.pallas_call(_chol_inv_kernel, out_shape=(jax.ShapeDtypeStruct((n, n),...  99.1 us
    dot_general x29, matrix products, times_t(): lax.dot_general(a, b, (((1,), (1,)), ((), ())), precision=HIGHEST, prefer...  50.1 us
    all_to_all x1, blocking collectives, row_sum(): received = lax.all_to_all(chunks, 'row', 0, 0)  37 us
    unnamed x134, local copies, waits for them, and re-layouts  27.9 us
    all_to_all x1, waiting for transfers between devices, row_sum(): return lax.all_to_all(spread, 'row', 0, 0).reshape(data.shape)  27 us
    ppermute x1, waiting for transfers between devices, shifted(): return lax.ppermute(array, axis, pairs)  14.4 us
    ppermute x1, waiting for transfers between devices, padded_2(): lax.ppermute(lax.slice_in_dim(block, block.shape[dim] - width, None, axis...  8.47 us
    mul x7, other arithmetic, body(): upper, inverse = chol_inv((block + block.T) * 0.5)  7.01 us
  transfers between devices with their start and end apart: 4, of which 4 were waited for; matrix products, arithmetic and copies ran while one was open for 2% of the time, Pallas kernels for 0%

profile of v3, /device:TPU:256, one launch (start us, length us, event | category | flops | bytes accessed | tf_op | source)
XLA Modules:
  0.0 325.7 jit_solution(8925396251827607064)
XLA Ops:
  2.0 3.5 %collective-permute-start = (bf16[256,1024]{1,0:T(8,128)(2,1)S(1)}, bf16[256,1024]{1,0:T(8,128)(2,1)S(1)}, u32[]{:S(2)}, u32[]{:S(2)}) collective-permute-start(bf16[256,1024]{1,0:T(8,128)(2,1)S(1)} %get-tuple-element.40), channel_id=1, source_target_pairs={{0,1},{1,2},{2,3},{3,4},{4,5},{5,6},{6,7},{7,8},{8,9},{9,10},{10,1... | collective-permute-start | bytes 1572872 | tf_op jit(solution)/shard_map/ppermute | solution.py:61
  5.5 5.7 %collective-permute-start.1 = (bf16[256,1024]{1,0:T(8,128)(2,1)S(1)}, bf16[256,1024]{1,0:T(8,128)(2,1)S(1)}, u32[]{:S(2)}, u32[]{:S(2)}) collective-permute-start(bf16[256,1024]{1,0:T(8,128)(2,1)S(1)} %get-tuple-element.41), channel_id=1, source_target_pairs={{1,0},{2,1},{3,2},{4,3},{5,4},{6,5},{7,6},{8,7},{9,8},{10,9},{11,1... | collective-permute-start | bytes 1572872 | tf_op jit(solution)/shard_map/ppermute | solution.py:64
  12.6 8.5 %collective-permute-done = bf16[256,1024]{1,0:T(8,128)(2,1)S(1)} collective-permute-done((bf16[256,1024]{1,0:T(8,128)(2,1)S(1)}, bf16[256,1024]{1,0:T(8,128)(2,1)S(1)}, u32[]{:S(2)}, u32[]{:S(2)}) %collective-permute-start) | collective-permute-done | bytes 524320 | tf_op jit(solution)/shard_map/ppermute | solution.py:61
  24.4 2.8 gather_fusion
  27.2 3.3 %bitcast_convert_fusion = bf16[8,1024,64]{1,2,0:T(8,128)(2,1)S(1)} fusion(bf16[8,4,64,1024]{3,2,1,0:T(8,128)(2,1)} %bitcast.173, pred[8,4]{1,0:T(8,128)(4,1)S(1)} %copy.42, bf16[8,64,4,64]{3,2,1,0:T(4,128)(2,1)S(1)} %copy-done.27), kind=kOutput, calls=%fused_computation.5 | convolution fusion | flops 271056896 | bytes 5505056 | tf_op jit(solution)/shard_map/rinj,rnjk->rik/dot_general | solution.py:138
  33.5 37.0 %all_to_all.10 = f32[16,288,128]{2,1,0:T(8,128)S(1)} all-to-all(f32[16,288,128]{2,1,0:T(8,128)S(1)} %bitcast.175), channel_id=1, replica_groups=mesh['seg'=32,'row'=16] {'row'}, dimensions={0} | all-to-all | bytes 4718592 | tf_op jit(solution)/shard_map/all_to_all | solution.py:112
  72.3 4.6 %all-to-all-start.1 = ((f32[16,288,128]{2,1,0:T(8,128)}), f32[16,288,128]{2,1,0:T(8,128)}, u32[]{:S(2)}, u32[]{:S(2)}) async-start(f32[16,288,128]{2,1,0:T(8,128)} %broadcast_in_dim.31), calls=%async_computation.1 | async-start | bytes 4718592 | tf_op jit(solution)/shard_map/all_to_all | solution.py:117
  80.4 27.0 %all-to-all-done.1 = f32[16,288,128]{2,1,0:T(8,128)} async-done(((f32[16,288,128]{2,1,0:T(8,128)}), f32[16,288,128]{2,1,0:T(8,128)}, u32[]{:S(2)}, u32[]{:S(2)}) %all-to-all-start.1) | async-done | bytes 2359328 | tf_op jit(solution)/shard_map/all_to_all | solution.py:117
  112.8 12.3 %shard_map.68 = (f32[128,128]{1,0:T(8,128)}, f32[128,128]{1,0:T(8,128)}) custom-call(f32[128,128]{1,0:T(8,128)} %get-tuple-element.39.a_ref), custom_call_target="tpu_custom_call" | custom-call | tf_op jit(solution)/shard_map/pallas_call | solution.py:41
  134.8 12.3 %shard_map.69 = (f32[128,128]{1,0:T(8,128)}, f32[128,128]{1,0:T(8,128)}) custom-call(f32[128,128]{1,0:T(8,128)} %fusion.87.a_ref), custom_call_target="tpu_custom_call" | custom-call | tf_op jit(solution)/shard_map/pallas_call | solution.py:41
  169.7 12.3 %shard_map.70 = (f32[128,128]{1,0:T(8,128)}, f32[128,128]{1,0:T(8,128)}) custom-call(f32[128,128]{1,0:T(8,128)} %fusion.86.a_ref), custom_call_target="tpu_custom_call" | custom-call | tf_op jit(solution)/shard_map/pallas_call | solution.py:41
  187.2 2.2 convolution_subtract_fusion.2
  189.4 2.2 convolution_subtract_fusion.8
  193.2 12.5 %shard_map.71 = (f32[128,128]{1,0:T(8,128)}, f32[128,128]{1,0:T(8,128)}) custom-call(f32[128,128]{1,0:T(8,128)} %fusion.85.a_ref), custom_call_target="tpu_custom_call" | custom-call | tf_op jit(solution)/shard_map/pallas_call | solution.py:41
  212.8 2.5 convolution_subtract_fusion.10
  217.0 12.3 %shard_map.72 = (f32[128,128]{1,0:T(8,128)}, f32[128,128]{1,0:T(8,128)}) custom-call(f32[128,128]{1,0:T(8,128)} %fusion.84.a_ref), custom_call_target="tpu_custom_call" | custom-call | tf_op jit(solution)/shard_map/pallas_call | solution.py:41
  238.4 2.2 convolution_subtract_fusion.11
  241.5 12.7 %shard_map.73 = (f32[128,128]{1,0:T(8,128)}, f32[128,128]{1,0:T(8,128)}) custom-call(f32[128,128]{1,0:T(8,128)} %fusion.83.a_ref), custom_call_target="tpu_custom_call" | custom-call | tf_op jit(solution)/shard_map/pallas_call | solution.py:41
  260.3 12.3 %shard_map.74 = (f32[128,128]{1,0:T(8,128)}, f32[128,128]{1,0:T(8,128)}) custom-call(f32[128,128]{1,0:T(8,128)} %fusion.82.a_ref), custom_call_target="tpu_custom_call" | custom-call | tf_op jit(solution)/shard_map/pallas_call | solution.py:41
  275.4 12.5 %shard_map.75 = (f32[128,128]{1,0:T(8,128)}, f32[128,128]{1,0:T(8,128)}) custom-call(f32[128,128]{1,0:T(8,128)} %fusion.81.a_ref), custom_call_target="tpu_custom_call" | custom-call | tf_op jit(solution)/shard_map/pallas_call | solution.py:41
  293.8 3.8 %convolution_subtract_fusion.4 = f32[512,128]{1,0:T(8,128)S(1)} fusion(f32[512,640]{0,1:T(8,128)} %get-tuple-element.46, f32[384,640]{0,1:T(8,128)} %get-tuple-element.69, f32[512,1024]{1,0:T(8,128)S(1)} %copy-done), kind=kOutput, calls=%fused_computation.18 | convolution fusion | flops 503382016 | bytes 2162688 | tf_op jit(solution)/shard_map/dot_general | solution.py:121
  298.8 4.0 %convolution_subtract_fusion.7 = f32[512,128]{1,0:T(8,128)S(1)} fusion(f32[512,768]{0,1:T(8,128)} %get-tuple-element.43, f32[256,768]{0,1:T(8,128)S(1)} %copy-done.17, f32[512,1024]{1,0:T(8,128)S(1)} %copy-done), kind=kOutput, calls=%fused_computation.21 | convolution fusion | flops 604045312 | bytes 2490368 | tf_op jit(solution)/shard_map/dot_general | solution.py:121
  303.3 3.1 convolution_subtract_fusion.3
  309.7 14.4 %collective-permute-done.2 = bf16[1,512,1024]{1,2,0:T(8,128)(2,1)S(1)} collective-permute-done((bf16[1,512,1024]{1,2,0:T(8,128)(2,1)S(1)}, bf16[1,512,1024]{1,2,0:T(8,128)(2,1)S(1)}, u32[]{:S(2)}, u32[]{:S(2)}) %collective-permute-start.2) | collective-permute-done | bytes 1048608 | tf_op jit(solution)/shard_map/ppermute | solution.py:72
  (227 shorter events, 98.1 us)
Async XLA Ops:
  0.6 22.4 %copy-start.16 = (bf16[1,512,1024]{2,1,0:T(8,128)(2,1)S(1)}, bf16[1,512,1024]{2,1,0:T(8,128)(2,1)}, u32[]{:S(2)}) copy-start(bf16[1,512,1024]{2,1,0:T(8,128)(2,1)} %param.5) | copy-start | bytes 3145732
  0.6 10.6 %copy-start.43 = (s32[1,8,4]{1,2,0:T(4,128)S(1)}, s32[1,8,4]{1,2,0:T(4,128)}, u32[]{:S(2)}) copy-start(s32[1,8,4]{1,2,0:T(4,128)} %param.8) | copy-start | bytes 388
  0.7 10.9 %copy-start.32 = (bf16[1,512,256]{2,1,0:T(8,128)(2,1)S(1)}, bf16[1,512,256]{2,1,0:T(8,128)(2,1)}, u32[]{:S(2)}) copy-start(bf16[1,512,256]{2,1,0:T(8,128)(2,1)} %param.7) | copy-start | bytes 786436
  2.0 19.0 %collective-permute-start = (bf16[256,1024]{1,0:T(8,128)(2,1)S(1)}, bf16[256,1024]{1,0:T(8,128)(2,1)S(1)}, u32[]{:S(2)}, u32[]{:S(2)}) collective-permute-start(bf16[256,1024]{1,0:T(8,128)(2,1)S(1)} %get-tuple-element.40), channel_id=1, source_target_pairs={{0,1},{1,2},{2,3},{3,4},{4,5},{5,6},{6,7},{7,8},{8,9},{9,10},{10,1... | collective-permute-start | bytes 1572872 | tf_op jit(solution)/shard_map/ppermute | solution.py:61
  5.5 16.7 %collective-permute-start.1 = (bf16[256,1024]{1,0:T(8,128)(2,1)S(1)}, bf16[256,1024]{1,0:T(8,128)(2,1)S(1)}, u32[]{:S(2)}, u32[]{:S(2)}) collective-permute-start(bf16[256,1024]{1,0:T(8,128)(2,1)S(1)} %get-tuple-element.41), channel_id=1, source_target_pairs={{1,0},{2,1},{3,2},{4,3},{5,4},{6,5},{7,6},{8,7},{9,8},{10,9},{11,1... | collective-permute-start | bytes 1572872 | tf_op jit(solution)/shard_map/ppermute | solution.py:64
  30.6 48.2 %copy-start.5 = (bf16[8,1024,64]{1,2,0:T(8,128)(2,1)}, bf16[8,1024,64]{1,2,0:T(8,128)(2,1)S(1)}, u32[]{:S(2)}) copy-start(bf16[8,1024,64]{1,2,0:T(8,128)(2,1)S(1)} %bitcast_convert_fusion) | copy-start | bytes 3145732
  72.3 35.1 %all-to-all-start.1 = ((f32[16,288,128]{2,1,0:T(8,128)}), f32[16,288,128]{2,1,0:T(8,128)}, u32[]{:S(2)}, u32[]{:S(2)}) async-start(f32[16,288,128]{2,1,0:T(8,128)} %broadcast_in_dim.31), calls=%async_computation.1 | async-start | bytes 4718592 | tf_op jit(solution)/shard_map/all_to_all | solution.py:117
  134.1 18.6 %copy-start.28 = (f32[256,128]{1,0:T(8,128)S(1)}, f32[256,128]{1,0:T(8,128)}, u32[]{:S(2)}) copy-start(f32[256,128]{1,0:T(8,128)} %slice.440) | copy-start | bytes 393220
  150.0 10.9 %copy-start = (f32[512,1024]{1,0:T(8,128)S(1)}, f32[512,1024]{1,0:T(8,128)}, u32[]{:S(2)}) copy-start(f32[512,1024]{1,0:T(8,128)} %bitcast_convert_fusion.1) | copy-start | bytes 6291460
  154.4 9.1 %copy-start.41 = (f32[128,128]{1,0:T(8,128)S(1)}, f32[128,128]{1,0:T(8,128)}, u32[]{:S(2)}) copy-start(f32[128,128]{1,0:T(8,128)} %get-tuple-element.27) | copy-start | bytes 196612
  166.4 39.3 %copy-start.1 = (f32[512,128]{0,1:T(8,128)}, f32[512,128]{0,1:T(8,128)S(1)}, u32[]{:S(2)}) copy-start(f32[512,128]{0,1:T(8,128)S(1)} %get-tuple-element.62) | copy-start | bytes 786436
  205.7 7.1 %copy-start.10 = (f32[512,128]{0,1:T(8,128)S(1)}, f32[512,128]{0,1:T(8,128)}, u32[]{:S(2)}) copy-start(f32[512,128]{0,1:T(8,128)} %slice.418) | copy-start | bytes 786436
  205.7 7.1 %copy-start.11 = (f32[512,128]{0,1:T(8,128)S(1)}, f32[512,128]{0,1:T(8,128)}, u32[]{:S(2)}) copy-start(f32[512,128]{0,1:T(8,128)} %slice.419) | copy-start | bytes 786436
  205.7 7.1 %copy-start.14 = (f32[512,128]{0,1:T(8,128)S(1)}, f32[512,128]{0,1:T(8,128)}, u32[]{:S(2)}) copy-start(f32[512,128]{0,1:T(8,128)} %copy-done.13) | copy-start | bytes 786436
  205.7 7.1 %copy-start.2 = (f32[512,128]{0,1:T(8,128)S(1)}, f32[512,128]{0,1:T(8,128)}, u32[]{:S(2)}) copy-start(f32[512,128]{0,1:T(8,128)} %copy-done.1) | copy-start | bytes 786436
  229.2 7.5 %copy-start.24 = (f32[512,128]{0,1:T(8,128)S(1)}, f32[512,128]{0,1:T(8,128)}, u32[]{:S(2)}) copy-start(f32[512,128]{0,1:T(8,128)} %copy-done.23) | copy-start | bytes 786436
  229.2 7.5 %copy-start.34 = (f32[128,128]{1,0:T(8,128)S(1)}, f32[128,128]{1,0:T(8,128)}, u32[]{:S(2)}) copy-start(f32[128,128]{1,0:T(8,128)} %get-tuple-element.22) | copy-start | bytes 196612
  236.1 21.4 %copy-start.29 = (f32[256,128]{0,1:T(8,128)S(1)}, f32[256,128]{0,1:T(8,128)}, u32[]{:S(2)}) copy-start(f32[256,128]{0,1:T(8,128)} %copy.83) | copy-start | bytes 393220
  240.7 33.0 %copy-start.33 = (f32[128,128]{0,1:T(8,128)S(1)}, f32[128,128]{0,1:T(8,128)}, u32[]{:S(2)}) copy-start(f32[128,128]{0,1:T(8,128)} %copy.84) | copy-start | bytes 196612
  257.5 32.3 %copy-start.3 = (f32[512,128]{0,1:T(8,128)S(1)}, f32[512,128]{0,1:T(8,128)}, u32[]{:S(2)}) copy-start(f32[512,128]{0,1:T(8,128)} %copy-done.1) | copy-start | bytes 786436
  259.6 31.2 %copy-start.15 = (f32[512,128]{0,1:T(8,128)S(1)}, f32[512,128]{0,1:T(8,128)}, u32[]{:S(2)}) copy-start(f32[512,128]{0,1:T(8,128)} %copy-done.13) | copy-start | bytes 786436
  273.7 18.1 %copy-start.20 = (f32[512,128]{0,1:T(8,128)S(1)}, f32[512,128]{0,1:T(8,128)}, u32[]{:S(2)}) copy-start(f32[512,128]{0,1:T(8,128)} %copy-done.19) | copy-start | bytes 786436
  303.3 20.9 %copy-start.12 = (bf16[512,1024]{0,1:T(8,128)(2,1)S(1)}, bf16[512,1024]{0,1:T(8,128)(2,1)}, u32[]{:S(2)}) copy-start(bf16[512,1024]{0,1:T(8,128)(2,1)} %copy.41) | copy-start | bytes 3145732
  306.8 17.3 %collective-permute-start.2 = (bf16[1,512,1024]{1,2,0:T(8,128)(2,1)S(1)}, bf16[1,512,1024]{1,2,0:T(8,128)(2,1)S(1)}, u32[]{:S(2)}, u32[]{:S(2)}) collective-permute-start(bf16[1,512,1024]{1,2,0:T(8,128)(2,1)S(1)} %fusion.7), channel_id=1, source_target_pairs={{0,16},{16,32},{32,48},{48,64},{64,80},{80,96},{96,112},{112,128},... | collective-permute-start | bytes 3145736 | tf_op jit(solution)/shard_map/ppermute | solution.py:72
  (28 other events, 124.8 us)

commit v4 on v3

--- a/solution.py
+++ b/solution.py
@@ -6,11 +6,13 @@
 from jax.experimental.pallas import tpu as pltpu
 
 
-def _chol_inv_kernel(a_ref, lt_ref, x_ref):
+def _chol_inv_kernel(a_ref, l_ref, x_ref, lt_ref):
     n = a_ref.shape[0]
     rows = 8
     nblk = n // rows
-    a = [a_ref[b * rows:(b + 1) * rows, :] for b in range(nblk)]
+    whole = a_ref[...]
+    whole = (whole + whole.T) * 0.5
+    a = [whole[b * rows:(b + 1) * rows, :] for b in range(nblk)]
     sub = lax.broadcasted_iota(jnp.int32, (rows, n), 0)
     lane1 = lax.broadcasted_iota(jnp.int32, (1, n), 1)
     x = [jnp.where(sub + b * rows == lax.broadcasted_iota(jnp.int32, (rows, n), 1), 1.0, 0.0).astype(jnp.float32)
@@ -34,6 +36,7 @@
                 x[b] = x[b] - col * xrow
     for b in range(nblk):
         x_ref[b * rows:(b + 1) * rows, :] = x[b]
+    l_ref[...] = lt_ref[...].T
 
 
 def chol_inv(a):
@@ -43,13 +46,15 @@
         out_shape=(jax.ShapeDtypeStruct((n, n), jnp.float32), jax.ShapeDtypeStruct((n, n), jnp.float32)),
         in_specs=[pl.BlockSpec(memory_space=pltpu.VMEM)],
         out_specs=(pl.BlockSpec(memory_space=pltpu.VMEM), pl.BlockSpec(memory_space=pltpu.VMEM)),
+        scratch_shapes=[pltpu.VMEM((n, n), jnp.float32)],
     )(a)
+
 
 BS = 64
 NB = 4
 REACH = 4
 PANEL = 128
-HIGHEST = lax.Precision.HIGHEST
+HIGH = lax.Precision.HIGH
 
 
 def padded_2(block, sides, width):
@@ -119,7 +124,7 @@
 
 def times_t(a, b):
     return lax.dot_general(
-        a, b, (((1,), (1,)), ((), ())), precision=HIGHEST, preferred_element_type=jnp.float32
+        a, b, (((1,), (1,)), ((), ())), precision=HIGH, preferred_element_type=jnp.float32
     )
 
 
@@ -166,9 +171,7 @@
                 [column[low - j * width:] for j, column in enumerate(columns)], axis=1
             )
             panel = panel - times_t(left, left[:width])
-        block = panel[:width]
-        upper, inverse = chol_inv((block + block.T) * 0.5)
-        diag = upper.T
+        diag, inverse = chol_inv(panel[:width])
         logs.append(jnp.log(jnp.sum(diag * eye, axis=0)))
         if low + width < col_count:
             below = times_t(panel[width:], inverse)

time: 332 us -> 316 us (0.952)
  other arithmetic: 20.2 us -> 11.1 us
  local copies, waits for them, and re-layouts: 44.6 us -> 38.5 us
    mul x7 -> x0, other arithmetic: 7.01 us -> none  [body(): upper, inverse = chol_inv((block + block.T) * 0.5)]
    unnamed x134 -> x126, local copies, waits for them, and re-layouts: 27.9 us -> 22.5 us
where the time goes in v4:
time: 316 us; the launch traced here: 310 us
  Pallas kernels  99.1 us (31%)
  matrix products  55.6 us (18%)
  waiting for transfers between devices  51.5 us (16%)
  local copies, waits for them, and re-layouts  38.5 us (12%)
  blocking collectives  37 us (12%)
  starting transfers between devices  15.7 us (5%)
  other arithmetic  11.1 us (4%)
    pallas_call x8, Pallas kernels, chol_inv(): pl.pallas_call(_chol_inv_kernel, out_shape=(jax.ShapeDtypeStruct((n, n),...  99.1 us
    dot_general x29, matrix products, times_t(): lax.dot_general(a, b, (((1,), (1,)), ((), ())), precision=HIGH, preferred...  49.4 us
    all_to_all x1, blocking collectives, row_sum(): received = lax.all_to_all(chunks, 'row', 0, 0)  37 us
    all_to_all x1, waiting for transfers between devices, row_sum(): return lax.all_to_all(spread, 'row', 0, 0).reshape(data.shape)  27.3 us
    unnamed x126, local copies, waits for them, and re-layouts  22.5 us
    ppermute x1, waiting for transfers between devices, shifted(): return lax.ppermute(array, axis, pairs)  14.6 us
    ppermute x1, waiting for transfers between devices, padded_2(): lax.ppermute(lax.slice_in_dim(block, block.shape[dim] - width, None, axis...  8.48 us
  transfers between devices with their start and end apart: 4, of which 4 were waited for; matrix products, arithmetic and copies ran while one was open for 2% of the time, Pallas kernels for 0%

profile of v4, /device:TPU:256, one launch (start us, length us, event | category | flops | bytes accessed | tf_op | source)
XLA Modules:
  0.0 310.2 jit_solution(15986532870537746760)
XLA Ops:
  2.0 3.5 %collective-permute-start = (bf16[256,1024]{1,0:T(8,128)(2,1)S(1)}, bf16[256,1024]{1,0:T(8,128)(2,1)S(1)}, u32[]{:S(2)}, u32[]{:S(2)}) collective-permute-start(bf16[256,1024]{1,0:T(8,128)(2,1)S(1)} %get-tuple-element.38), channel_id=1, source_target_pairs={{0,1},{1,2},{2,3},{3,4},{4,5},{5,6},{6,7},{7,8},{8,9},{9,10},{10,1... | collective-permute-start | bytes 1572872 | tf_op jit(solution)/shard_map/ppermute | solution.py:66
  5.5 5.7 %collective-permute-start.1 = (bf16[256,1024]{1,0:T(8,128)(2,1)S(1)}, bf16[256,1024]{1,0:T(8,128)(2,1)S(1)}, u32[]{:S(2)}, u32[]{:S(2)}) collective-permute-start(bf16[256,1024]{1,0:T(8,128)(2,1)S(1)} %get-tuple-element.39), channel_id=1, source_target_pairs={{1,0},{2,1},{3,2},{4,3},{5,4},{6,5},{7,6},{8,7},{9,8},{10,9},{11,1... | collective-permute-start | bytes 1572872 | tf_op jit(solution)/shard_map/ppermute | solution.py:69
  12.6 8.5 %collective-permute-done = bf16[256,1024]{1,0:T(8,128)(2,1)S(1)} collective-permute-done((bf16[256,1024]{1,0:T(8,128)(2,1)S(1)}, bf16[256,1024]{1,0:T(8,128)(2,1)S(1)}, u32[]{:S(2)}, u32[]{:S(2)}) %collective-permute-start) | collective-permute-done | bytes 524320 | tf_op jit(solution)/shard_map/ppermute | solution.py:66
  24.4 2.8 gather_fusion
  27.2 3.3 %bitcast_convert_fusion = bf16[8,1024,64]{1,2,0:T(8,128)(2,1)S(1)} fusion(bf16[8,4,64,1024]{3,2,1,0:T(8,128)(2,1)} %bitcast.109, pred[8,4]{1,0:T(8,128)(4,1)S(1)} %copy.13, bf16[8,64,4,64]{3,2,1,0:T(4,128)(2,1)S(1)} %copy-done.29), kind=kOutput, calls=%fused_computation.5 | convolution fusion | flops 271056896 | bytes 5505056 | tf_op jit(solution)/shard_map/rinj,rnjk->rik/dot_general | solution.py:143
  33.5 37.0 %all_to_all.10 = f32[16,288,128]{2,1,0:T(8,128)S(1)} all-to-all(f32[16,288,128]{2,1,0:T(8,128)S(1)} %bitcast.111), channel_id=1, replica_groups=mesh['seg'=32,'row'=16] {'row'}, dimensions={0} | all-to-all | bytes 4718592 | tf_op jit(solution)/shard_map/all_to_all | solution.py:117
  72.3 4.6 %all-to-all-start.1 = ((f32[16,288,128]{2,1,0:T(8,128)}), f32[16,288,128]{2,1,0:T(8,128)}, u32[]{:S(2)}, u32[]{:S(2)}) async-start(f32[16,288,128]{2,1,0:T(8,128)} %broadcast_in_dim.31), calls=%async_computation.1 | async-start | bytes 4718592 | tf_op jit(solution)/shard_map/all_to_all | solution.py:122
  80.1 27.3 %all-to-all-done.1 = f32[16,288,128]{2,1,0:T(8,128)} async-done(((f32[16,288,128]{2,1,0:T(8,128)}), f32[16,288,128]{2,1,0:T(8,128)}, u32[]{:S(2)}, u32[]{:S(2)}) %all-to-all-start.1) | async-done | bytes 2359328 | tf_op jit(solution)/shard_map/all_to_all | solution.py:122
  109.9 12.4 %shard_map.68 = (f32[128,128]{1,0:T(8,128)}, f32[128,128]{1,0:T(8,128)}) custom-call(f32[128,128]{1,0:T(8,128)} %slice.399.a_ref), custom_call_target="tpu_custom_call" | custom-call | tf_op jit(solution)/shard_map/pallas_call | solution.py:44
  129.5 12.4 %shard_map.69 = (f32[128,128]{1,0:T(8,128)}, f32[128,128]{1,0:T(8,128)}) custom-call(f32[128,128]{1,0:T(8,128)} %slice.404.a_ref), custom_call_target="tpu_custom_call" | custom-call | tf_op jit(solution)/shard_map/pallas_call | solution.py:44
  151.6 2.5 convolution_subtract_fusion.5
  154.7 12.4 %shard_map.70 = (f32[128,128]{1,0:T(8,128)}, f32[128,128]{1,0:T(8,128)}) custom-call(f32[128,128]{1,0:T(8,128)} %slice.409.a_ref), custom_call_target="tpu_custom_call" | custom-call | tf_op jit(solution)/shard_map/pallas_call | solution.py:44
  174.2 2.6 convolution_subtract_fusion.8
  177.4 12.4 %shard_map.71 = (f32[128,128]{1,0:T(8,128)}, f32[128,128]{1,0:T(8,128)}) custom-call(f32[128,128]{1,0:T(8,128)} %slice.415.a_ref), custom_call_target="tpu_custom_call" | custom-call | tf_op jit(solution)/shard_map/pallas_call | solution.py:44
  194.5 2.6 convolution_subtract_fusion.9
  197.2 2.7 convolution_subtract_fusion.10
  200.5 12.4 %shard_map.72 = (f32[128,128]{1,0:T(8,128)}, f32[128,128]{1,0:T(8,128)}) custom-call(f32[128,128]{1,0:T(8,128)} %slice.422.a_ref), custom_call_target="tpu_custom_call" | custom-call | tf_op jit(solution)/shard_map/pallas_call | solution.py:44
  227.1 12.4 %shard_map.73 = (f32[128,128]{1,0:T(8,128)}, f32[128,128]{1,0:T(8,128)}) custom-call(f32[128,128]{1,0:T(8,128)} %slice.431.a_ref), custom_call_target="tpu_custom_call" | custom-call | tf_op jit(solution)/shard_map/pallas_call | solution.py:44
  245.5 12.4 %shard_map.74 = (f32[128,128]{1,0:T(8,128)}, f32[128,128]{1,0:T(8,128)}) custom-call(f32[128,128]{1,0:T(8,128)} %slice.441.a_ref), custom_call_target="tpu_custom_call" | custom-call | tf_op jit(solution)/shard_map/pallas_call | solution.py:44
  262.6 12.4 %shard_map.75 = (f32[128,128]{1,0:T(8,128)}, f32[128,128]{1,0:T(8,128)}) custom-call(f32[128,128]{1,0:T(8,128)} %convolution_subtract_fusion.13.a_ref), custom_call_target="tpu_custom_call" | custom-call | tf_op jit(solution)/shard_map/pallas_call | solution.py:44
  280.7 2.8 convolution_subtract_fusion.4
  284.6 3.0 convolution_subtract_fusion.7
  288.1 2.8 convolution_subtract_fusion.3
  294.0 14.6 %collective-permute-done.2 = bf16[1,512,1024]{1,2,0:T(8,128)(2,1)S(1)} collective-permute-done((bf16[1,512,1024]{1,2,0:T(8,128)(2,1)S(1)}, bf16[1,512,1024]{1,2,0:T(8,128)(2,1)S(1)}, u32[]{:S(2)}, u32[]{:S(2)}) %collective-permute-start.2) | collective-permute-done | bytes 1048608 | tf_op jit(solution)/shard_map/ppermute | solution.py:77
  (198 shorter events, 83.2 us)
Async XLA Ops:
  0.6 22.4 %copy-start.17 = (bf16[1,512,1024]{2,1,0:T(8,128)(2,1)S(1)}, bf16[1,512,1024]{2,1,0:T(8,128)(2,1)}, u32[]{:S(2)}) copy-start(bf16[1,512,1024]{2,1,0:T(8,128)(2,1)} %param.5) | copy-start | bytes 3145732
  0.6 10.6 %copy-start.43 = (s32[1,8,4]{1,2,0:T(4,128)S(1)}, s32[1,8,4]{1,2,0:T(4,128)}, u32[]{:S(2)}) copy-start(s32[1,8,4]{1,2,0:T(4,128)} %param.8) | copy-start | bytes 388
  0.7 10.9 %copy-start.32 = (bf16[1,512,256]{2,1,0:T(8,128)(2,1)S(1)}, bf16[1,512,256]{2,1,0:T(8,128)(2,1)}, u32[]{:S(2)}) copy-start(bf16[1,512,256]{2,1,0:T(8,128)(2,1)} %param.7) | copy-start | bytes 786436
  2.0 19.0 %collective-permute-start = (bf16[256,1024]{1,0:T(8,128)(2,1)S(1)}, bf16[256,1024]{1,0:T(8,128)(2,1)S(1)}, u32[]{:S(2)}, u32[]{:S(2)}) collective-permute-start(bf16[256,1024]{1,0:T(8,128)(2,1)S(1)} %get-tuple-element.38), channel_id=1, source_target_pairs={{0,1},{1,2},{2,3},{3,4},{4,5},{5,6},{6,7},{7,8},{8,9},{9,10},{10,1... | collective-permute-start | bytes 1572872 | tf_op jit(solution)/shard_map/ppermute | solution.py:66
  5.5 16.7 %collective-permute-start.1 = (bf16[256,1024]{1,0:T(8,128)(2,1)S(1)}, bf16[256,1024]{1,0:T(8,128)(2,1)S(1)}, u32[]{:S(2)}, u32[]{:S(2)}) collective-permute-start(bf16[256,1024]{1,0:T(8,128)(2,1)S(1)} %get-tuple-element.39), channel_id=1, source_target_pairs={{1,0},{2,1},{3,2},{4,3},{5,4},{6,5},{7,6},{8,7},{9,8},{10,9},{11,1... | collective-permute-start | bytes 1572872 | tf_op jit(solution)/shard_map/ppermute | solution.py:69
  30.5 47.9 %copy-start.7 = (bf16[8,1024,64]{1,2,0:T(8,128)(2,1)}, bf16[8,1024,64]{1,2,0:T(8,128)(2,1)S(1)}, u32[]{:S(2)}) copy-start(bf16[8,1024,64]{1,2,0:T(8,128)(2,1)S(1)} %bitcast_convert_fusion) | copy-start | bytes 3145732
  72.3 35.1 %all-to-all-start.1 = ((f32[16,288,128]{2,1,0:T(8,128)}), f32[16,288,128]{2,1,0:T(8,128)}, u32[]{:S(2)}, u32[]{:S(2)}) async-start(f32[16,288,128]{2,1,0:T(8,128)} %broadcast_in_dim.31), calls=%async_computation.1 | async-start | bytes 4718592 | tf_op jit(solution)/shard_map/all_to_all | solution.py:122
  127.6 19.2 %copy-start.40 = (f32[128,128]{1,0:T(8,128)S(1)}, f32[128,128]{1,0:T(8,128)}, u32[]{:S(2)}) copy-start(f32[128,128]{1,0:T(8,128)} %get-tuple-element.26) | copy-start | bytes 196612
  143.3 5.9 %copy-start.6 = (f32[768,128]{0,1:T(8,128)S(1)}, f32[768,128]{0,1:T(8,128)}, u32[]{:S(2)}) copy-start(f32[768,128]{0,1:T(8,128)} %slice.406) | copy-start | bytes 1179652
  189.8 7.3 %copy-start.4 = (f32[512,128]{0,1:T(8,128)S(1)}, f32[512,128]{0,1:T(8,128)}, u32[]{:S(2)}) copy-start(f32[512,128]{0,1:T(8,128)} %copy-done.2) | copy-start | bytes 786436
  189.8 7.4 %copy-start.10 = (f32[512,128]{0,1:T(8,128)S(1)}, f32[512,128]{0,1:T(8,128)}, u32[]{:S(2)}) copy-start(f32[512,128]{0,1:T(8,128)} %slice.417) | copy-start | bytes 786436
  189.8 7.4 %copy-start.11 = (f32[512,128]{0,1:T(8,128)S(1)}, f32[512,128]{0,1:T(8,128)}, u32[]{:S(2)}) copy-start(f32[512,128]{0,1:T(8,128)} %slice.418) | copy-start | bytes 786436
  189.8 7.4 %copy-start.12 = (f32[512,128]{0,1:T(8,128)S(1)}, f32[512,128]{0,1:T(8,128)}, u32[]{:S(2)}) copy-start(f32[512,128]{0,1:T(8,128)} %slice.419) | copy-start | bytes 786436
  189.8 7.4 %copy-start.15 = (f32[512,128]{0,1:T(8,128)S(1)}, f32[512,128]{0,1:T(8,128)}, u32[]{:S(2)}) copy-start(f32[512,128]{0,1:T(8,128)} %copy-done.14) | copy-start | bytes 786436
  191.1 8.7 %copy-start = (f32[512,128]{0,1:T(8,128)}, f32[512,128]{0,1:T(8,128)S(1)}, u32[]{:S(2)}) copy-start(f32[512,128]{0,1:T(8,128)S(1)} %fusion.54) | copy-start | bytes 786436
  200.5 20.8 %copy-start.1 = (f32[512,128]{0,1:T(8,128)S(1)}, f32[512,128]{0,1:T(8,128)}, u32[]{:S(2)}) copy-start(f32[512,128]{0,1:T(8,128)} %copy-done) | copy-start | bytes 786436
  212.9 9.1 %copy-start.26 = (f32[512,128]{1,0:T(8,128)S(1)}, f32[512,128]{1,0:T(8,128)}, u32[]{:S(2)}) copy-start(f32[512,128]{1,0:T(8,128)} %copy-done.25) | copy-start | bytes 786436
  212.9 9.1 %copy-start.35 = (f32[128,128]{1,0:T(8,128)S(1)}, f32[128,128]{1,0:T(8,128)}, u32[]{:S(2)}) copy-start(f32[128,128]{1,0:T(8,128)} %get-tuple-element.22) | copy-start | bytes 196612
  226.5 48.5 %copy-start.28 = (f32[512,128]{1,0:T(8,128)S(1)}, f32[512,128]{1,0:T(8,128)}, u32[]{:S(2)}) copy-start(f32[512,128]{1,0:T(8,128)} %convolution_subtract_fusion.10) | copy-start | bytes 786436
  240.9 35.9 %copy-start.5 = (f32[512,128]{0,1:T(8,128)S(1)}, f32[512,128]{0,1:T(8,128)}, u32[]{:S(2)}) copy-start(f32[512,128]{0,1:T(8,128)} %copy-done.2) | copy-start | bytes 786436
  242.7 35.1 %copy-start.16 = (f32[512,128]{0,1:T(8,128)S(1)}, f32[512,128]{0,1:T(8,128)}, u32[]{:S(2)}) copy-start(f32[512,128]{0,1:T(8,128)} %copy-done.14) | copy-start | bytes 786436
  258.5 20.2 %copy-start.21 = (f32[512,128]{0,1:T(8,128)S(1)}, f32[512,128]{0,1:T(8,128)}, u32[]{:S(2)}) copy-start(f32[512,128]{0,1:T(8,128)} %copy-done.20) | copy-start | bytes 786436
  288.0 20.5 %copy-start.13 = (bf16[512,1024]{0,1:T(8,128)(2,1)S(1)}, bf16[512,1024]{0,1:T(8,128)(2,1)}, u32[]{:S(2)}) copy-start(bf16[512,1024]{0,1:T(8,128)(2,1)} %copy.12) | copy-start | bytes 3145732
  291.2 17.3 %collective-permute-start.2 = (bf16[1,512,1024]{1,2,0:T(8,128)(2,1)S(1)}, bf16[1,512,1024]{1,2,0:T(8,128)(2,1)S(1)}, u32[]{:S(2)}, u32[]{:S(2)}) collective-permute-start(bf16[1,512,1024]{1,2,0:T(8,128)(2,1)S(1)} %fusion.7), channel_id=1, source_target_pairs={{0,16},{16,32},{32,48},{48,64},{64,80},{80,96},{96,112},{112,128},... | collective-permute-start | bytes 3145736 | tf_op jit(solution)/shard_map/ppermute | solution.py:77
  (28 other events, 113.1 us)
